TPU v7x, 32 devices: a whole 2x2x4 slice. The times are simulated.
32 devices in a mesh: pipe: 2 (over core), ep: 16 (over z, y, x).
Axes of the slice: x: 2, y: 2, z: 4, core: 2. Of those that a mesh axis runs over, the one named last changes fastest.
Arguments:
- x_fwd: bfloat16 [2, 1024, 2048], P('pipe', 'ep'), may hold values from -6 to 6
- ids_fwd: int32 [2, 1024, 8], P('pipe', 'ep'), may hold values from 0 to 15, all different within a row; in each aligned block of 64 rows (0 to 63, 64 to 127, ..., all dimensions but the last counted through in order) at most 48 rows name the same one
- route_fwd: float32 [2, 1024, 8], P('pipe', 'ep'), may hold values from 0.05 to 1
- x_bwd: bfloat16 [2, 1024, 2048], P('pipe', 'ep'), may hold values from -6 to 6
- grad_bwd: bfloat16 [2, 1024, 2048], P('pipe', 'ep'), may hold values from -6 to 6
- ids_bwd: int32 [2, 1024, 8], P('pipe', 'ep'), may hold values from 0 to 15, all different within a row; in each aligned block of 64 rows (0 to 63, 64 to 127, ..., all dimensions but the last counted through in order) at most 48 rows name the same one
- route_bwd: float32 [2, 1024, 8], P('pipe', 'ep'), may hold values from 0.05 to 1
- norm_gain: bfloat16 [2, 2048], P('pipe'), may hold values from 0.25 to 1.75
- w_gate: bfloat16 [2, 16, 2048, 768], P('pipe', 'ep'), may hold values from -0.125 to 0.125
- w_up: bfloat16 [2, 16, 2048, 768], P('pipe', 'ep'), may hold values from -0.125 to 0.125
- w_down: bfloat16 [2, 16, 768, 2048], P('pipe', 'ep'), may hold values from -0.21875 to 0.21875
Outputs:
- fwd_next: bfloat16 [2, 1024, 2048], P('pipe', 'ep')
- bwd_prev: bfloat16 [2, 1024, 2048], P('pipe', 'ep')
Inputs may be any that keep to these rules, and one draw needn't show every extreme that they name: `ids_fwd`: in each aligned block of 64 tokens of a section, each token names 8 different experts, no expert is named by more than 48 tokens, and in some block one expert is named by exactly 48. `ids_bwd`: as for ids_fwd.
All inputs are finite; a program needn't handle non-finite values.
Results may differ from a plain program's by a relative error of at most 0.0046.
Values may be sent and summed in bfloat16 or wider, within the bound.
No kernel may reach another device: no remote copies, remote signals or barrier semaphores. Data moves between devices by JAX's collectives and lax.ppermute only.
A program may use at most 128 MiB of HBM per device.

v0:
```python
import jax
import jax.numpy as jnp
from jax import lax
from jax.sharding import PartitionSpec as P

EPS = 1e-06


def from_behind(block, axis, distance):
    devices = range(lax.axis_size(axis))
    route = [((i - distance) % len(devices), i) for i in devices]
    return lax.ppermute(block, axis, route)


def slot_places(ids, n_exp, cap):
    flat = ids.reshape(-1)
    onehot = (flat[:, None] == jnp.arange(n_exp, dtype=jnp.int32)[None, :]).astype(jnp.int32)
    before = jnp.cumsum(onehot, axis=0) - onehot
    slot = jnp.sum(before * onehot, axis=1)
    return flat * cap + slot


def rms_stats(x):
    xf = x.astype(jnp.float32)
    scale = lax.rsqrt(jnp.mean(xf * xf, axis=-1, keepdims=True) + EPS)
    return (xf, scale)


def expert_forward(rows, w_g, w_u, w_d):
    gate = jnp.dot(rows, w_g, preferred_element_type=jnp.float32)
    upper = jnp.dot(rows, w_u, preferred_element_type=jnp.float32)
    act = (jax.nn.silu(gate) * upper).astype(jnp.bfloat16)
    return jnp.dot(act, w_d, preferred_element_type=jnp.float32).astype(jnp.bfloat16)


def expert_backward(rows, cot, w_g, w_u, w_d):
    gate = jnp.dot(rows, w_g, preferred_element_type=jnp.float32)
    upper = jnp.dot(rows, w_u, preferred_element_type=jnp.float32)
    sigma = jax.nn.sigmoid(gate)
    dact = jnp.dot(cot, w_d.T, preferred_element_type=jnp.float32)
    dgate = (dact * upper * sigma * (1.0 + gate * (1.0 - sigma))).astype(jnp.bfloat16)
    dup = (dact * gate * sigma).astype(jnp.bfloat16)
    total = jnp.dot(dgate, w_g.T, preferred_element_type=jnp.float32) + jnp.dot(
        dup, w_u.T, preferred_element_type=jnp.float32
    )
    return total.astype(jnp.bfloat16)


def norm_backward(xf, scale, gain, upstream):
    scaled = gain * upstream
    inner = jnp.mean(xf * scaled, axis=-1, keepdims=True)
    return scale * scaled - xf * (scale * scale * scale) * inner


def route_layout(ids, route, n_exp, cap):
    top = ids.shape[1]
    places = slot_places(ids, n_exp, cap)
    count = places.shape[0]
    source = (
        jnp.full((n_exp * cap,), -1, jnp.int32).at[places].set(jnp.arange(count, dtype=jnp.int32))
    )
    valid = (source >= 0)[:, None]
    safe = jnp.maximum(source, 0)
    weights = route / jnp.sum(route, axis=-1, keepdims=True)
    return (places, valid, safe // top, weights.reshape(-1)[safe], weights)


def local(
    x_fwd, ids_fwd, route_fwd, x_bwd, grad_bwd, ids_bwd, route_bwd, norm_gain, w_gate, w_up, w_down
):
    n_exp = lax.axis_size("ep")
    tok_dev = x_fwd.shape[1]
    width = x_fwd.shape[2]
    top = ids_fwd.shape[2]
    cap = 3 * tok_dev * top // (2 * n_exp)
    gain = norm_gain[0].astype(jnp.float32)
    w_g = w_gate[0, 0]
    w_u = w_up[0, 0]
    w_d = w_down[0, 0]
    zero_b = jnp.zeros((), jnp.bfloat16)
    xf, scale_f = rms_stats(x_fwd[0])
    h_f = (xf * scale_f * gain).astype(jnp.bfloat16)
    xb, scale_b = rms_stats(x_bwd[0])
    h_b = (xb * scale_b * gain).astype(jnp.bfloat16)
    grad = grad_bwd[0]
    places_f, valid_f, token_f, slot_w_f, weights_f = route_layout(
        ids_fwd[0], route_fwd[0], n_exp, cap
    )
    places_b, valid_b, token_b, slot_w_b, weights_b = route_layout(
        ids_bwd[0], route_bwd[0], n_exp, cap
    )
    send_f = jnp.where(valid_f, h_f[token_f], zero_b).reshape(n_exp, cap, width)
    send_b = jnp.where(valid_b, h_b[token_b], zero_b).reshape(n_exp, cap, width)
    cot_rows = (slot_w_b[:, None] * grad[token_b].astype(jnp.float32)).astype(jnp.bfloat16)
    send_g = jnp.where(valid_b, cot_rows, zero_b).reshape(n_exp, cap, width)
    got_f, got_b, got_g = (
        lax.all_to_all(send_f, "ep", split_axis=0, concat_axis=0, tiled=True),
        lax.all_to_all(send_b, "ep", split_axis=0, concat_axis=0, tiled=True),
        lax.all_to_all(send_g, "ep", split_axis=0, concat_axis=0, tiled=True),
    )
    rows = got_f.reshape(-1, width)
    made_f = expert_forward(rows, w_g, w_u, w_d).reshape(got_f.shape)
    rows = got_b.reshape(-1, width)
    cots = got_g.reshape(-1, width)
    made_b = expert_backward(rows, cots, w_g, w_u, w_d).reshape(got_b.shape)
    back_f, back_b = (
        lax.all_to_all(made_f, "ep", split_axis=0, concat_axis=0, tiled=True),
        lax.all_to_all(made_b, "ep", split_axis=0, concat_axis=0, tiled=True),
    )
    picked_f = back_f.reshape(-1, width)[places_f].reshape(tok_dev, top, width)
    mixed = jnp.sum(weights_f[:, :, None] * picked_f.astype(jnp.float32), axis=1)
    layer_out = (xf + mixed).astype(jnp.bfloat16)[None]
    picked_b = back_b.reshape(-1, width)[places_b].reshape(tok_dev, top, width)
    dnorm = jnp.sum(picked_b.astype(jnp.float32), axis=1)
    input_grad = (grad.astype(jnp.float32) + norm_backward(xb, scale_b, gain, dnorm)).astype(
        jnp.bfloat16
    )[None]
    fwd_next = from_behind(layer_out, "pipe", 1)
    bwd_prev = from_behind(input_grad, "pipe", -1)
    return (fwd_next, bwd_prev)


def solution(mesh):
    placed = (
        P("pipe", "ep", None),
        P("pipe", "ep", None),
        P("pipe", "ep", None),
        P("pipe", "ep", None),
        P("pipe", "ep", None),
        P("pipe", "ep", None),
        P("pipe", "ep", None),
        P("pipe", None),
        P("pipe", "ep", None, None),
        P("pipe", "ep", None, None),
        P("pipe", "ep", None, None),
    )
    return jax.shard_map(
        local,
        mesh=mesh,
        in_specs=placed,
        out_specs=(P("pipe", "ep", None), P("pipe", "ep", None)),
        check_vma=False,
    )
```

profile of v0, /device:TPU:13, one launch (start us, length us, event | category | flops | bytes accessed | tf_op | source)
XLA Modules:
  0.0 494.8 jit_solution(5898736921196354198)
XLA Ops:
  0.6 0.9 copy.20
  1.6 0.1 eq.62
  1.7 0.1 eq.58
  1.7 0.7 broadcast_multiply_fusion
  2.4 1.1 reduce-window.16
  3.6 0.2 slice_reduce_fusion
  3.9 0.1 copy.19
  3.9 0.1 mul.204
  4.0 0.1 fusion.46
  4.2 2.4 scatter_custom_fusion.1
  6.6 0.7 mul.228
  7.3 1.1 fusion.35
  8.5 1.8 fusion.37
  10.3 8.2 %gather_fusion.4 = bf16[768,2048]{1,0:T(8,128)(2,1)} fusion(bf16[64,2048]{1,0:T(8,128)(2,1)} %fusion.37, s32[1024]{0:T(1024)S(1)} %get-tuple-element.10), kind=kCustom, calls=%fused_computation.4 | custom fusion | bytes 6294528 | tf_op jit(solution)/shard_map/gather | solution.py:93
  18.5 4.3 gather_fusion.3
  22.8 0.1 copy.23
  22.9 0.1 div.58
  23.0 0.1 div.59
  23.1 0.1 squeeze.25
  23.2 5.0 %gather_fusion.2 = f32[768]{0:T(1024)S(1)} fusion(f32[512]{0:T(512)S(1)} %div.60, s32[1024]{0:T(1024)S(1)} %get-tuple-element.11), kind=kCustom, calls=%fused_computation.2 | custom fusion | bytes 9216 | tf_op jit(solution)/shard_map/gather | solution.py:65
  28.2 0.1 mul.206
  28.2 0.1 broadcast_in_dim.60
  28.3 5.1 %fusion.2 = (bf16[16,48,2048]{2,1,0:T(8,128)(2,1)}, bf16[16,48,2048]{2,1,0:T(8,128)(2,1)S(1)}) fusion(bf16[16,48,2048]{2,1,0:T(8,128)(2,1)} %bitcast.134, f32[16,48]{1,0:T(8,128)S(1)} %mul.206, pred[16,48]{1,0:T(8,128)(4,1)S(1)} %broadcast_in_dim.60, bf16[16,48,2048]{2,1,0:T(8,128)(2,1)} %bitcast.133), kind=kLoop, calls=%fused_computation.15 | loop fusion | flops 7864320 | bytes 12586752 | tf_op jit(solution)/shard_map/jit(_where)/select_n | solution.py:95
  33.5 76.1 %all_to_all.25 = bf16[16,48,2048]{2,1,0:T(8,128)(2,1)} all-to-all(bf16[16,48,2048]{2,1,0:T(8,128)(2,1)S(1)} %get-tuple-element.7), channel_id=1, replica_groups=mesh['pipe'=2,'ep'=16] {'ep'}, dimensions={0} | all-to-all | bytes 6291456 | tf_op jit(solution)/shard_map/all_to_all | solution.py:98
  109.6 5.2 %all-to-all-start.2 = ((bf16[16,48,2048]{2,1,0:T(8,128)(2,1)}), bf16[16,48,2048]{2,1,0:T(8,128)(2,1)}, u32[]{:S(2)}, u32[]{:S(2)}) async-start(bf16[16,48,2048]{2,1,0:T(8,128)(2,1)} %get-tuple-element.6), calls=%async_computation.2 | async-start | bytes 6291456 | tf_op jit(solution)/shard_map/all_to_all | solution.py:99
  114.8 6.8 %fusion.13 = f32[768,768]{1,0:T(8,128)} fusion(bf16[768,2048]{1,0:T(8,128)(2,1)} %bitcast.137, bf16[1,1,2048,768]{3,2,1,0:T(8,128)(2,1)} %param.19), kind=kOutput, calls=%fused_computation.26 | convolution fusion | flops 2415919104 | bytes 8650752 | tf_op jit(solution)/shard_map/dot_general | solution.py:37
  121.6 63.6 %all-to-all-done.2 = bf16[16,48,2048]{2,1,0:T(8,128)(2,1)} async-done(((bf16[16,48,2048]{2,1,0:T(8,128)(2,1)}), bf16[16,48,2048]{2,1,0:T(8,128)(2,1)}, u32[]{:S(2)}, u32[]{:S(2)}) %all-to-all-start.2) | async-done | bytes 3145760 | tf_op jit(solution)/shard_map/all_to_all | solution.py:99
  185.2 7.0 %fusion.3 = f32[768,768]{1,0:T(8,128)} fusion(bf16[768,2048]{1,0:T(8,128)(2,1)} %bitcast.21, bf16[1,1,768,2048]{3,2,1,0:T(8,128)(2,1)} %param.21), kind=kOutput, calls=%fused_computation.16 | convolution fusion | flops 2415919104 | bytes 8650752 | tf_op jit(solution)/shard_map/dot_general | solution.py:40
  192.2 12.7 %fusion.11 = f32[768,2048]{1,0:T(8,128)} fusion(bf16[1,1,2048,768]{3,2,1,0:T(8,128)(2,1)} %param.19, f32[768,768]{1,0:T(8,128)} %fusion.13, f32[768,768]{1,0:T(8,128)} %fusion.3, bf16[768,2048]{1,0:T(8,128)(2,1)} %bitcast.138, bf16[1,1,2048,768]{3,2,1,0:T(8,128)(2,1)S(1)} %copy-done), kind=kOutput, calls=%fused_computation.24 | convolution fusion | flops 4837736448 | bytes 20447232 | tf_op jit(solution)/shard_map/dot_general | solution.py:43
  204.9 7.4 %add_convert_fusion = bf16[768,2048]{1,0:T(8,128)(2,1)} fusion(f32[768,2048]{1,0:T(8,128)} %fusion.11, bf16[1,1,2048,768]{3,2,1,0:T(8,128)(2,1)S(1)} %copy-done, f32[768,768]{1,0:T(8,128)} %fusion.3, f32[768,768]{1,0:T(8,128)} %fusion.13), kind=kOutput, calls=%fused_computation.10 | convolution fusion | flops 2422603776 | bytes 17301504 | tf_op jit(solution)/shard_map/dot_general | solution.py:43
  212.4 4.5 all-to-all-start.4
  216.9 0.1 copy.16
  217.0 0.1 eq.54
  217.1 0.1 eq.50
  217.2 1.2 reduce-window.14
  218.3 0.2 slice_reduce_fusion.1
  218.6 0.1 copy.15
  218.7 0.1 mul.188
  218.8 0.1 fusion.49
  218.9 2.7 scatter_custom_fusion
  221.6 0.1 broadcast_in_dim.56
  221.7 1.1 fusion.31
  222.8 64.4 %all-to-all-done.4 = bf16[16,48,2048]{2,1,0:T(8,128)(2,1)} async-done(((bf16[16,48,2048]{2,1,0:T(8,128)(2,1)}), bf16[16,48,2048]{2,1,0:T(8,128)(2,1)}, u32[]{:S(2)}, u32[]{:S(2)}) %all-to-all-start.4) | async-done | bytes 3145760 | tf_op jit(solution)/shard_map/all_to_all | solution.py:108
  287.2 7.5 %gather_fusion.5 = bf16[512,2048]{1,0:T(8,128)(2,1)} fusion(bf16[768,2048]{1,0:T(8,128)(2,1)} %bitcast.25, s32[1024]{0:T(1024)S(1)} %pad_clamp_fusion), kind=kCustom, calls=%fused_computation.5 | custom fusion | bytes 4196352 | tf_op jit(solution)/shard_map/gather | solution.py:113
  294.7 3.0 convert_reduce_fusion
  297.8 0.8 copy-done.2
  298.6 2.0 fusion.38
  300.6 8.1 %gather_fusion = bf16[768,2048]{1,0:T(8,128)(2,1)} fusion(bf16[64,2048]{1,0:T(8,128)(2,1)} %get-tuple-element.3, s32[1024]{0:T(1024)S(1)} %pad_clamp_fusion.4), kind=kCustom, calls=%fused_computation | custom fusion | bytes 6294528 | tf_op jit(solution)/shard_map/gather | solution.py:92
  308.7 2.2 broadcast_select_fusion.1
  310.8 74.1 %all_to_all.26 = bf16[16,48,2048]{2,1,0:T(8,128)(2,1)S(1)} all-to-all(bf16[16,48,2048]{2,1,0:T(8,128)(2,1)S(1)} %broadcast_select_fusion.1), channel_id=1, replica_groups=mesh['pipe'=2,'ep'=16] {'ep'}, dimensions={0} | all-to-all | bytes 6291456 | tf_op jit(solution)/shard_map/all_to_all | solution.py:97
  384.9 1.7 copy-done.3
  386.6 4.0 fusion.9
  390.6 11.9 %convolution_convert_fusion = bf16[768,2048]{1,0:T(8,128)(2,1)} fusion(bf16[1,1,768,2048]{3,2,1,0:T(8,128)(2,1)} %param.21, f32[768,768]{1,0:T(8,128)} %fusion.9, bf16[768,2048]{1,0:T(8,128)(2,1)} %bitcast.140, bf16[1,1,2048,768]{3,2,1,0:T(8,128)(2,1)} %param.19), kind=kOutput, calls=%fused_computation.14 | convolution fusion | flops 4836950016 | bytes 14942208 | tf_op jit(solution)/shard_map/dot_general | solution.py:33
  402.5 5.0 %all-to-all-start.1 = ((bf16[16,48,2048]{2,1,0:T(8,128)(2,1)}), bf16[16,48,2048]{2,1,0:T(8,128)(2,1)}, u32[]{:S(2)}, u32[]{:S(2)}) async-start(bf16[16,48,2048]{2,1,0:T(8,128)(2,1)} %bitcast.136), calls=%async_computation.1 | async-start | bytes 6291456 | tf_op jit(solution)/shard_map/all_to_all | solution.py:107
  407.6 0.1 copy.14
  407.7 2.1 fusion.42
  409.8 2.4 collective-permute-start.1
  412.2 66.0 %all-to-all-done.1 = bf16[16,48,2048]{2,1,0:T(8,128)(2,1)} async-done(((bf16[16,48,2048]{2,1,0:T(8,128)(2,1)}), bf16[16,48,2048]{2,1,0:T(8,128)(2,1)}, u32[]{:S(2)}, u32[]{:S(2)}) %all-to-all-start.1) | async-done | bytes 3145760 | tf_op jit(solution)/shard_map/all_to_all | solution.py:107
  478.2 7.6 %gather_fusion.1 = bf16[512,2048]{1,0:T(8,128)(2,1)} fusion(bf16[768,2048]{1,0:T(8,128)(2,1)} %bitcast.12, s32[1024]{0:T(1024)S(1)} %pad_clamp_fusion.3), kind=kCustom, calls=%fused_computation.1 | custom fusion | bytes 4196352 | tf_op jit(solution)/shard_map/gather | solution.py:110
  485.8 3.4 fusion.1
  489.3 1.5 collective-permute-start
  490.8 1.2 collective-permute-done
  492.0 0.7 copy.30
  492.7 1.7 copy.31
  (42 shorter events, 0.3 us)
Async XLA Ops:
  0.6 191.5 %copy-start = (bf16[1,1,2048,768]{3,2,1,0:T(8,128)(2,1)S(1)}, bf16[1,1,2048,768]{3,2,1,0:T(8,128)(2,1)}, u32[]{:S(2)}) copy-start(bf16[1,1,2048,768]{3,2,1,0:T(8,128)(2,1)} %param.20) | copy-start | bytes 9437188
  10.3 8.2 %copy-start.1 = (bf16[1,64,2048]{2,1,0:T(8,128)(2,1)S(1)}, bf16[1,64,2048]{2,1,0:T(8,128)(2,1)}, u32[]{:S(2)}) copy-start(bf16[1,64,2048]{2,1,0:T(8,128)(2,1)} %param.15) | copy-start | bytes 786436
  18.5 4.3 copy-start.5
  109.6 75.6 %all-to-all-start.2 = ((bf16[16,48,2048]{2,1,0:T(8,128)(2,1)}), bf16[16,48,2048]{2,1,0:T(8,128)(2,1)}, u32[]{:S(2)}, u32[]{:S(2)}) async-start(bf16[16,48,2048]{2,1,0:T(8,128)(2,1)} %get-tuple-element.6), calls=%async_computation.2 | async-start | bytes 6291456 | tf_op jit(solution)/shard_map/all_to_all | solution.py:99
  212.4 4.5 copy-start.6
  212.4 74.9 %all-to-all-start.4 = ((bf16[16,48,2048]{2,1,0:T(8,128)(2,1)}), bf16[16,48,2048]{2,1,0:T(8,128)(2,1)}, u32[]{:S(2)}, u32[]{:S(2)}) async-start(bf16[16,48,2048]{2,1,0:T(8,128)(2,1)} %bitcast.135), calls=%async_computation.4 | async-start | bytes 6291456 | tf_op jit(solution)/shard_map/all_to_all | solution.py:108
  297.7 0.8 copy-start.2
  384.9 1.7 copy-start.3
  402.5 5.1 %copy-start.7 = (f32[1,64,8]{1,2,0:T(8,128)S(1)}, f32[1,64,8]{1,2,0:T(8,128)}, u32[]{:S(2)}) copy-start(f32[1,64,8]{1,2,0:T(8,128)} %param.13) | copy-start | bytes 6148
  402.5 75.6 %all-to-all-start.1 = ((bf16[16,48,2048]{2,1,0:T(8,128)(2,1)}), bf16[16,48,2048]{2,1,0:T(8,128)(2,1)}, u32[]{:S(2)}, u32[]{:S(2)}) async-start(bf16[16,48,2048]{2,1,0:T(8,128)(2,1)} %bitcast.136), calls=%async_computation.1 | async-start | bytes 6291456 | tf_op jit(solution)/shard_map/all_to_all | solution.py:107
  409.8 81.0 %collective-permute-start.1 = (bf16[1,64,2048]{2,1,0:T(8,128)(2,1)}, bf16[1,64,2048]{2,1,0:T(8,128)(2,1)}, u32[]{:S(2)}, u32[]{:S(2)}) collective-permute-start(bf16[1,64,2048]{2,1,0:T(8,128)(2,1)} %fusion.42), channel_id=1, source_target_pairs={{16,0},{0,16},{17,1},{1,17},{18,2},{2,18},{19,3},{3,19},{20,4},{4,... | collective-permute-start | bytes 786440 | tf_op jit(solution)/shard_map/ppermute | solution.py:12
  478.2 11.1 %copy-start.4 = (bf16[1,64,2048]{2,1,0:T(8,128)(2,1)S(1)}, bf16[1,64,2048]{2,1,0:T(8,128)(2,1)}, u32[]{:S(2)}) copy-start(bf16[1,64,2048]{2,1,0:T(8,128)(2,1)} %param.11) | copy-start | bytes 786436
  489.3 2.6 collective-permute-start
where the time goes:
time: 501 us; the launch traced here: 495 us
  waiting for transfers between devices  195 us (39%)
  blocking collectives  150 us (30%)
  local copies, waits for them, and re-layouts  53.6 us (11%)
  matrix products  49.9 us (10%)
  other arithmetic  25.9 us (5%)
  starting transfers between devices  18.6 us (4%)
    all_to_all x1, blocking collectives, local(): lax.all_to_all(send_b, 'ep', split_axis=0, concat_axis=0, tiled=True)  76.1 us
    all_to_all x1, blocking collectives, local(): lax.all_to_all(send_f, 'ep', split_axis=0, concat_axis=0, tiled=True)  74.1 us
    all_to_all x1, waiting for transfers between devices, local(): lax.all_to_all(made_f, 'ep', split_axis=0, concat_axis=0, tiled=True)  66 us
    all_to_all x1, waiting for transfers between devices, local(): lax.all_to_all(made_b, 'ep', split_axis=0, concat_axis=0, tiled=True)  64.4 us
    all_to_all x1, waiting for transfers between devices, local(): lax.all_to_all(send_g, 'ep', split_axis=0, concat_axis=0, tiled=True)  63.6 us
    dot_general x1, matrix products, expert_backward(): jnp.dot(dgate, w_g.T, preferred_element_type=jnp.float32)  12.7 us
    dot_general x1, matrix products, expert_forward(): jnp.dot(act, w_d, preferred_element_type=jnp.float32).astype(jnp.bfloat16)  11.9 us
  transfers between devices with their start and end apart: 5, of which 4 were waited for; matrix products, arithmetic and copies ran while one was open for 5% of the time, Pallas kernels for 0%

commit v1 on v0

--- a/solution.py
+++ b/solution.py
@@ -52,23 +52,34 @@
     return scale * scaled - xf * (scale * scale * scale) * inner
 
 
-def route_layout(ids, route, n_exp, cap):
-    top = ids.shape[1]
-    places = slot_places(ids, n_exp, cap)
-    count = places.shape[0]
-    source = (
-        jnp.full((n_exp * cap,), -1, jnp.int32).at[places].set(jnp.arange(count, dtype=jnp.int32))
-    )
-    valid = (source >= 0)[:, None]
-    safe = jnp.maximum(source, 0)
-    weights = route / jnp.sum(route, axis=-1, keepdims=True)
-    return (places, valid, safe // top, weights.reshape(-1)[safe], weights)
+def expert_slots(ids_all, weights_all, me, cap):
+    match = ids_all == me
+    chosen = jnp.any(match, axis=-1)
+    weight = jnp.sum(jnp.where(match, weights_all, 0.0), axis=-1)
+    pos = jnp.cumsum(chosen.astype(jnp.int32), axis=1) - chosen.astype(jnp.int32)
+    slot = jnp.arange(cap, dtype=jnp.int32)[None, :, None]
+    onehot = chosen[:, None, :] & (pos[:, None, :] == slot)
+    slot_w = jnp.sum(jnp.where(onehot, weight[:, None, :], 0.0), axis=-1)
+    return onehot.astype(jnp.bfloat16), slot_w
+
+
+def pick_rows(onehot, rows):
+    picked = jnp.einsum("bct,btd->bcd", onehot, rows, preferred_element_type=jnp.float32)
+    return picked.astype(jnp.bfloat16)
+
+
+def combine_rows(places, back, top):
+    count = back.shape[0]
+    onehot = (places[:, None] == jnp.arange(count, dtype=jnp.int32)[None, :]).astype(jnp.bfloat16)
+    picked = jnp.dot(onehot, back, preferred_element_type=jnp.float32)
+    return picked.reshape(-1, top, back.shape[1])
 
 
 def local(
     x_fwd, ids_fwd, route_fwd, x_bwd, grad_bwd, ids_bwd, route_bwd, norm_gain, w_gate, w_up, w_down
 ):
     n_exp = lax.axis_size("ep")
+    me = lax.axis_index("ep")
     tok_dev = x_fwd.shape[1]
     width = x_fwd.shape[2]
     top = ids_fwd.shape[2]
@@ -77,41 +88,44 @@
     w_g = w_gate[0, 0]
     w_u = w_up[0, 0]
     w_d = w_down[0, 0]
-    zero_b = jnp.zeros((), jnp.bfloat16)
     xf, scale_f = rms_stats(x_fwd[0])
     h_f = (xf * scale_f * gain).astype(jnp.bfloat16)
     xb, scale_b = rms_stats(x_bwd[0])
     h_b = (xb * scale_b * gain).astype(jnp.bfloat16)
     grad = grad_bwd[0]
-    places_f, valid_f, token_f, slot_w_f, weights_f = route_layout(
-        ids_fwd[0], route_fwd[0], n_exp, cap
-    )
-    places_b, valid_b, token_b, slot_w_b, weights_b = route_layout(
-        ids_bwd[0], route_bwd[0], n_exp, cap
-    )
-    send_f = jnp.where(valid_f, h_f[token_f], zero_b).reshape(n_exp, cap, width)
-    send_b = jnp.where(valid_b, h_b[token_b], zero_b).reshape(n_exp, cap, width)
-    cot_rows = (slot_w_b[:, None] * grad[token_b].astype(jnp.float32)).astype(jnp.bfloat16)
-    send_g = jnp.where(valid_b, cot_rows, zero_b).reshape(n_exp, cap, width)
-    got_f, got_b, got_g = (
-        lax.all_to_all(send_f, "ep", split_axis=0, concat_axis=0, tiled=True),
-        lax.all_to_all(send_b, "ep", split_axis=0, concat_axis=0, tiled=True),
-        lax.all_to_all(send_g, "ep", split_axis=0, concat_axis=0, tiled=True),
-    )
-    rows = got_f.reshape(-1, width)
-    made_f = expert_forward(rows, w_g, w_u, w_d).reshape(got_f.shape)
-    rows = got_b.reshape(-1, width)
-    cots = got_g.reshape(-1, width)
-    made_b = expert_backward(rows, cots, w_g, w_u, w_d).reshape(got_b.shape)
-    back_f, back_b = (
-        lax.all_to_all(made_f, "ep", split_axis=0, concat_axis=0, tiled=True),
-        lax.all_to_all(made_b, "ep", split_axis=0, concat_axis=0, tiled=True),
-    )
-    picked_f = back_f.reshape(-1, width)[places_f].reshape(tok_dev, top, width)
-    mixed = jnp.sum(weights_f[:, :, None] * picked_f.astype(jnp.float32), axis=1)
+    weights_f = route_fwd[0] / jnp.sum(route_fwd[0], axis=-1, keepdims=True)
+    weights_b = route_bwd[0] / jnp.sum(route_bwd[0], axis=-1, keepdims=True)
+
+    def gather(v):
+        return lax.all_gather(v, "ep", axis=0, tiled=False)
+
+    all_h_f = gather(h_f)
+    all_ids_f = gather(ids_fwd[0])
+    all_w_f = gather(weights_f)
+    all_h_b = gather(h_b)
+    all_g = gather(grad)
+    all_ids_b = gather(ids_bwd[0])
+    all_w_b = gather(weights_b)
+
+    onehot_f, _ = expert_slots(all_ids_f, all_w_f, me, cap)
+    rows = pick_rows(onehot_f, all_h_f).reshape(-1, width)
+    made_f = expert_forward(rows, w_g, w_u, w_d).reshape(n_exp, cap, width)
+    back_f = lax.all_to_all(made_f, "ep", split_axis=0, concat_axis=0, tiled=True)
+
+    onehot_b, slot_w_b = expert_slots(all_ids_b, all_w_b, me, cap)
+    rows = pick_rows(onehot_b, all_h_b).reshape(-1, width)
+    g_rows = pick_rows(onehot_b, all_g)
+    cots = (slot_w_b[:, :, None] * g_rows.astype(jnp.float32)).astype(jnp.bfloat16).reshape(-1, width)
+    made_b = expert_backward(rows, cots, w_g, w_u, w_d).reshape(n_exp, cap, width)
+    back_b = lax.all_to_all(made_b, "ep", split_axis=0, concat_axis=0, tiled=True)
+
+    places_f = slot_places(ids_fwd[0], n_exp, cap)
+    picked_f = combine_rows(places_f, back_f.reshape(-1, width), top)
+    mixed = jnp.sum(weights_f[:, :, None] * picked_f, axis=1)
     layer_out = (xf + mixed).astype(jnp.bfloat16)[None]
-    picked_b = back_b.reshape(-1, width)[places_b].reshape(tok_dev, top, width)
-    dnorm = jnp.sum(picked_b.astype(jnp.float32), axis=1)
+    places_b = slot_places(ids_bwd[0], n_exp, cap)
+    picked_b = combine_rows(places_b, back_b.reshape(-1, width), top)
+    dnorm = jnp.sum(picked_b, axis=1)
     input_grad = (grad.astype(jnp.float32) + norm_backward(xb, scale_b, gain, dnorm)).astype(
         jnp.bfloat16
     )[None]

time: 501 us -> 462 us (0.922); the launches traced: 495 us -> 461 us
  waiting for transfers between devices: 195 us -> 277 us
  blocking collectives: 150 us -> 77.6 us
  local copies, waits for them, and re-layouts: 53.6 us -> 7.04 us
  other arithmetic: 25.9 us -> 10 us
  matrix products: 49.9 us -> 62.8 us
  between operations: 1.34 us -> 14 us
  starting transfers between devices: 18.6 us -> 13.3 us
    all_to_all x2 -> x0, blocking collectives: 150 us -> none  [the longest x1 76.1 us: local(): lax.all_to_all(send_b, 'ep', split_axis=0, concat_axis=0, tiled=True)]
    all_gather x0 -> x3, waiting for transfers between devices: none -> 140 us  [gather(): return lax.all_gather(v, 'ep', axis=0, tiled=False)]
    all_gather x0 -> x3, blocking collectives: none -> 77.6 us  [gather(): return lax.all_gather(v, 'ep', axis=0, tiled=False)]
    all_to_all x1 -> x0, waiting for transfers between devices: 63.6 us -> none  [local(): lax.all_to_all(send_g, 'ep', split_axis=0, concat_axis=0, tiled=True)]
    gather x6 -> x0, local copies, waits for them, and re-layouts: 40.8 us -> none  [the longest x1 8.22 us: local(): send_b = jnp.where(valid_b, h_b[token_b], zero_b).reshape(n_exp, cap, width)]
    dot_general x0 -> x5, matrix products: none -> 18.5 us  [the longest x3 9.72 us: pick_rows(): jnp.einsum('bct,btd->bcd', onehot, rows, preferred_element_type=jnp.float32)]
    select_n x5 -> x0, other arithmetic: 7.32 us -> none  [the longest x1 5.13 us: local(): send_g = jnp.where(valid_b, cot_rows, zero_b).reshape(n_exp, cap, width)]
    reduce_sum x4, other arithmetic: 6.47 us -> 0.94 us  [the longest x1 0.71 us: local(): weights_b = route_bwd[0] / jnp.sum(route_bwd[0], axis=-1, keepdims=True)]
  transfers between devices with their start and end apart: 5 -> 7, of which waited for: 4 -> 6; matrix products, arithmetic and copies ran while one was open for 5% -> 5% of each run, Pallas kernels for 0% -> 0%
where the time goes in v1:
time: 462 us; the launch traced here: 461 us
  waiting for transfers between devices  277 us (60%)
  blocking collectives  77.6 us (17%)
  matrix products  62.8 us (14%)
  between operations  14 us (3%)
  starting transfers between devices  13.3 us (3%)
  other arithmetic  10 us (2%)
  local copies, waits for them, and re-layouts  7.04 us (2%)
    all_gather x3, waiting for transfers between devices, gather(): return lax.all_gather(v, 'ep', axis=0, tiled=False)  140 us
    all_gather x3, blocking collectives, gather(): return lax.all_gather(v, 'ep', axis=0, tiled=False)  77.6 us
    all_to_all x1, waiting for transfers between devices, local(): lax.all_to_all(made_b, 'ep', split_axis=0, concat_axis=0, tiled=True)  68.5 us
    all_to_all x1, waiting for transfers between devices, local(): lax.all_to_all(made_f, 'ep', split_axis=0, concat_axis=0, tiled=True)  66.4 us
    dot_general x1, matrix products, expert_backward(): jnp.dot(dgate, w_g.T, preferred_element_type=jnp.float32)  12.7 us
    dot_general x1, matrix products, expert_forward(): jnp.dot(act, w_d, preferred_element_type=jnp.float32).astype(jnp.bfloat16)  11.9 us
    dot_general x3, matrix products, pick_rows(): jnp.einsum('bct,btd->bcd', onehot, rows, preferred_element_type=jnp.float32)  9.72 us
  transfers between devices with their start and end apart: 7, of which 6 were waited for; matrix products, arithmetic and copies ran while one was open for 5% of the time, Pallas kernels for 0%

profile of v1, /device:TPU:13, one launch (start us, length us, event | category | flops | bytes accessed | tf_op | source)
XLA Modules:
  0.0 461.4 jit_solution(9350285513648293935)
XLA Ops:
  7.2 0.0 copy-start
  7.2 0.0 all-gather.6.cloned.1.call-start
  7.2 0.7 all-gather.6.cloned.1.call-update
  7.9 0.0 all-gather.8.cloned.1.call-start
  8.0 0.9 mul.219
  8.8 1.1 fusion.31
  9.9 1.8 fusion.38
  11.7 0.0 all-gather.8.cloned.1.call-update
  11.8 0.7 reduce_sum.116
  12.5 0.7 broadcast_divide_fusion
  13.2 25.1 %all_gather.24 = f32[16,64,8]{1,2,0:T(8,128)S(1)} all-gather(f32[1,64,8]{1,2,0:T(8,128)S(1)} %broadcast_divide_fusion), channel_id=1, replica_groups=mesh['pipe'=2,'ep'=16] {'ep'}, dimensions={0}, use_global_device_ids=true | all-gather | bytes 34816 | tf_op jit(solution)/shard_map/all_gather | solution.py:100
  38.2 29.9 %all_gather.23 = s32[16,64,8]{1,2,0:T(8,128)S(1)} all-gather(s32[1,64,8]{1,2,0:T(8,128)} %param.16), channel_id=1, replica_groups=mesh['pipe'=2,'ep'=16] {'ep'}, dimensions={0}, use_global_device_ids=true | all-gather | bytes 34816 | tf_op jit(solution)/shard_map/all_gather | solution.py:100
  68.3 0.2 reduce_window_sum.47
  68.5 0.2 select_reduce_fusion
  68.7 18.2 %all-gather.6.cloned.1.call-done = bf16[16,64,2048]{2,1,0:T(8,128)(2,1)} async-done(((bf16[1,64,2048]{2,1,0:T(8,128)(2,1)}), bf16[16,64,2048]{2,1,0:T(8,128)(2,1)}) %all-gather.6.cloned.1.call-update) | async-done | bytes 4194320 | tf_op jit(solution)/shard_map/all_gather | solution.py:100
  86.9 3.3 multiply_convert_fusion
  90.2 4.0 fusion
  94.3 70.5 %all-gather.8.cloned.1.call-done = bf16[16,64,2048]{2,1,0:T(8,128)(2,1)} async-done(((bf16[1,64,2048]{2,1,0:T(8,128)(2,1)}), bf16[16,64,2048]{2,1,0:T(8,128)(2,1)}) %all-gather.8.cloned.1.call-update) | async-done | bytes 4194320 | tf_op jit(solution)/shard_map/all_gather | solution.py:100
  164.7 3.3 convolution_convert_fusion
  168.0 1.7 copy-done.2
  169.7 4.1 fusion.10
  173.9 12.7 %fusion.8 = f32[768,2048]{1,0:T(8,128)} fusion(bf16[1,1,2048,768]{3,2,1,0:T(8,128)(2,1)} %param.19, f32[768,768]{1,0:T(8,128)} %fusion.10, f32[768,768]{1,0:T(8,128)} %fusion, bf16[768,2048]{1,0:T(8,128)(2,1)} %bitcast.118, bf16[1,1,2048,768]{3,2,1,0:T(8,128)(2,1)S(1)} %copy-done), kind=kOutput, calls=%fused_computation.15 | convolution fusion | flops 4837736448 | bytes 20447232 | tf_op jit(solution)/shard_map/dot_general | solution.py:43
  186.6 7.4 %add_convert_fusion = bf16[768,2048]{1,0:T(8,128)(2,1)} fusion(f32[768,2048]{1,0:T(8,128)} %fusion.8, bf16[1,1,2048,768]{3,2,1,0:T(8,128)(2,1)S(1)} %copy-done, f32[768,768]{1,0:T(8,128)} %fusion, f32[768,768]{1,0:T(8,128)} %fusion.10), kind=kOutput, calls=%fused_computation | convolution fusion | flops 2422603776 | bytes 17301504 | tf_op jit(solution)/shard_map/dot_general | solution.py:43
  194.1 4.9 %all-to-all-start.1 = ((bf16[16,48,2048]{2,1,0:T(8,128)(2,1)}), bf16[16,48,2048]{2,1,0:T(8,128)(2,1)}, u32[]{:S(2)}, u32[]{:S(2)}) async-start(bf16[16,48,2048]{2,1,0:T(8,128)(2,1)} %bitcast.122), calls=%async_computation.1 | async-start | bytes 6291456 | tf_op jit(solution)/shard_map/all_to_all | solution.py:120
  198.9 0.0 all-gather.4.cloned.1.call-start
  199.0 0.1 copy.30
  199.1 0.1 eq.165
  199.2 0.1 eq.161
  199.3 1.2 reduce-window.16
  200.4 0.2 slice_reduce_fusion
  200.7 0.1 fusion.57
  200.8 0.1 reduce_sum.115
  200.9 0.2 fusion.33
  201.1 68.5 %all-to-all-done.1 = bf16[16,48,2048]{2,1,0:T(8,128)(2,1)} async-done(((bf16[16,48,2048]{2,1,0:T(8,128)(2,1)}), bf16[16,48,2048]{2,1,0:T(8,128)(2,1)}, u32[]{:S(2)}, u32[]{:S(2)}) %all-to-all-start.1) | async-done | bytes 3145760 | tf_op jit(solution)/shard_map/all_to_all | solution.py:120
  269.5 4.4 convolution_reduce_fusion
  273.9 0.2 fusion.32
  274.1 0.0 copy-done.5
  274.1 1.1 fusion.42
  275.2 0.0 all-gather.4.cloned.1.call-update
  275.2 22.6 %all_gather.21 = s32[16,64,8]{1,2,0:T(8,128)S(1)} all-gather(s32[1,64,8]{1,2,0:T(8,128)S(1)} %copy-done.7), channel_id=1, replica_groups=mesh['pipe'=2,'ep'=16] {'ep'}, dimensions={0}, use_global_device_ids=true | all-gather | bytes 34816 | tf_op jit(solution)/shard_map/all_gather | solution.py:100
  297.8 0.2 reduce_window_sum.44
  298.0 51.3 %all-gather.4.cloned.1.call-done = bf16[16,64,2048]{2,1,0:T(8,128)(2,1)} async-done(((bf16[1,64,2048]{2,1,0:T(8,128)(2,1)}), bf16[16,64,2048]{2,1,0:T(8,128)(2,1)}) %all-gather.4.cloned.1.call-update) | async-done | bytes 4194320 | tf_op jit(solution)/shard_map/all_gather | solution.py:100
  349.3 3.1 convolution_convert_fusion.3
  352.5 1.7 copy-done.3
  354.2 4.0 fusion.6
  358.2 11.9 %convolution_convert_fusion.2 = bf16[768,2048]{1,0:T(8,128)(2,1)} fusion(bf16[1,1,768,2048]{3,2,1,0:T(8,128)(2,1)} %param.21, f32[768,768]{1,0:T(8,128)} %fusion.6, bf16[768,2048]{1,0:T(8,128)(2,1)} %bitcast.120, bf16[1,1,2048,768]{3,2,1,0:T(8,128)(2,1)} %param.19), kind=kOutput, calls=%fused_computation.5 | convolution fusion | flops 4836950016 | bytes 14942208 | tf_op jit(solution)/shard_map/dot_general | solution.py:33
  370.1 4.7 %all-to-all-start = ((bf16[16,48,2048]{2,1,0:T(8,128)(2,1)}), bf16[16,48,2048]{2,1,0:T(8,128)(2,1)}, u32[]{:S(2)}, u32[]{:S(2)}) async-start(bf16[16,48,2048]{2,1,0:T(8,128)(2,1)} %bitcast.121), calls=%async_computation | async-start | bytes 6291456 | tf_op jit(solution)/shard_map/all_to_all | solution.py:113
  374.8 0.1 copy.26
  374.9 0.1 eq.148
  375.0 0.1 eq.144
  375.1 1.2 reduce-window.14
  376.3 0.2 slice_reduce_fusion.1
  376.5 0.1 fusion.60
  376.6 0.1 reduce_sum.109
  376.8 0.1 copy.25
  376.9 2.1 collective-permute-start.1
  379.0 66.4 %all-to-all-done = bf16[16,48,2048]{2,1,0:T(8,128)(2,1)} async-done(((bf16[16,48,2048]{2,1,0:T(8,128)(2,1)}), bf16[16,48,2048]{2,1,0:T(8,128)(2,1)}, u32[]{:S(2)}, u32[]{:S(2)}) %all-to-all-start) | async-done | bytes 3145760 | tf_op jit(solution)/shard_map/all_to_all | solution.py:113
  445.4 4.4 multiply_reduce_fusion
  449.8 0.1 fusion.36
  449.9 1.5 collective-permute-start
  451.4 0.0 collective-permute-done.1
  451.4 1.2 collective-permute-done
  452.5 0.7 copy.40
  453.2 1.7 copy.41
  (38 shorter events, 0.3 us)
Async XLA Ops:
  7.2 166.7 %copy-start = (bf16[1,1,2048,768]{3,2,1,0:T(8,128)(2,1)S(1)}, bf16[1,1,2048,768]{3,2,1,0:T(8,128)(2,1)}, u32[]{:S(2)}) copy-start(bf16[1,1,2048,768]{3,2,1,0:T(8,128)(2,1)} %param.20) | copy-start | bytes 9437188
  7.2 79.7 %all-gather.6.cloned.1.call-start = ((), (), s32[]{:S(2)}) async-start(), calls=%async_computation.3 | async-start | bytes 4456448 | tf_op jit(solution)/shard_map/all_gather | solution.py:100
  7.9 156.8 %all-gather.8.cloned.1.call-start = ((), (), s32[]{:S(2)}) async-start(), calls=%async_computation.4 | async-start | bytes 4456448 | tf_op jit(solution)/shard_map/all_gather | solution.py:100
  86.9 3.3 copy-start.9
  164.7 5.0 %copy-start.10 = (bf16[1,1,2048,768]{3,2,1,0:T(8,128)(2,1)S(1)}, bf16[1,1,2048,768]{3,2,1,0:T(8,128)(2,1)}, u32[]{:S(2)}) copy-start(bf16[1,1,2048,768]{3,2,1,0:T(8,128)(2,1)} %param.19) | copy-start | bytes 9437188
  168.0 1.7 copy-start.2
  194.1 4.9 %copy-start.6 = (s32[1,64,8]{1,2,0:T(8,128)S(1)}, s32[1,64,8]{1,2,0:T(8,128)}, u32[]{:S(2)}) copy-start(s32[1,64,8]{1,2,0:T(8,128)} %param.16) | copy-start | bytes 6148
  194.1 6.8 %copy-start.4 = (bf16[1,64,2048]{2,1,0:T(8,128)(2,1)S(1)}, bf16[1,64,2048]{2,1,0:T(8,128)(2,1)}, u32[]{:S(2)}) copy-start(bf16[1,64,2048]{2,1,0:T(8,128)(2,1)} %param.11) | copy-start | bytes 786436
  194.1 75.5 %all-to-all-start.1 = ((bf16[16,48,2048]{2,1,0:T(8,128)(2,1)}), bf16[16,48,2048]{2,1,0:T(8,128)(2,1)}, u32[]{:S(2)}, u32[]{:S(2)}) async-start(bf16[16,48,2048]{2,1,0:T(8,128)(2,1)} %bitcast.122), calls=%async_computation.1 | async-start | bytes 6291456 | tf_op jit(solution)/shard_map/all_to_all | solution.py:120
  198.9 150.4 %all-gather.4.cloned.1.call-start = ((), (), s32[]{:S(2)}) async-start(), calls=%async_computation.2 | async-start | bytes 4456448 | tf_op jit(solution)/shard_map/all_gather | solution.py:100
  269.5 4.4 copy-start.1
  269.5 4.6 copy-start.5
  269.5 5.7 %copy-start.7 = (s32[1,64,8]{1,2,0:T(8,128)S(1)}, s32[1,64,8]{1,2,0:T(8,128)}, u32[]{:S(2)}) copy-start(s32[1,64,8]{1,2,0:T(8,128)} %param.12) | copy-start | bytes 6148
  352.5 1.7 copy-start.3
  370.1 6.6 %copy-start.8 = (f32[1,64,8]{1,2,0:T(8,128)S(1)}, f32[1,64,8]{1,2,0:T(8,128)}, u32[]{:S(2)}) copy-start(f32[1,64,8]{1,2,0:T(8,128)} %param.13) | copy-start | bytes 6148
  370.1 75.3 %all-to-all-start = ((bf16[16,48,2048]{2,1,0:T(8,128)(2,1)}), bf16[16,48,2048]{2,1,0:T(8,128)(2,1)}, u32[]{:S(2)}, u32[]{:S(2)}) async-start(bf16[16,48,2048]{2,1,0:T(8,128)(2,1)} %bitcast.121), calls=%async_computation | async-start | bytes 6291456 | tf_op jit(solution)/shard_map/all_to_all | solution.py:113
  376.9 74.5 %collective-permute-start.1 = (bf16[1,64,2048]{2,1,0:T(8,128)(2,1)}, bf16[1,64,2048]{2,1,0:T(8,128)(2,1)}, u32[]{:S(2)}, u32[]{:S(2)}) collective-permute-start(bf16[1,64,2048]{2,1,0:T(8,128)(2,1)} %get-tuple-element.4), channel_id=1, source_target_pairs={{16,0},{0,16},{17,1},{1,17},{18,2},{2,18},{19,3},{3,19},{20,4},{4,... | collective-permute-start | bytes 786440 | tf_op jit(solution)/shard_map/ppermute | solution.py:12
  449.9 2.6 collective-permute-start
Sparse Core Ops, SparseCore 0:
  10.8 76.1 all-gather.5
  90.3 74.4 all-gather.7
  275.3 73.9 all-gather.3

commit v2 on v1

--- a/solution.py
+++ b/solution.py
@@ -99,13 +99,21 @@
     def gather(v):
         return lax.all_gather(v, "ep", axis=0, tiled=False)
 
+    tables = gather(
+        jnp.concatenate(
+            [ids_fwd[0].astype(jnp.float32), route_fwd[0], ids_bwd[0].astype(jnp.float32), route_bwd[0]],
+            axis=-1,
+        )
+    )
+    all_ids_f = tables[..., 0:top].astype(jnp.int32)
+    all_route_f = tables[..., top:2 * top]
+    all_ids_b = tables[..., 2 * top:3 * top].astype(jnp.int32)
+    all_route_b = tables[..., 3 * top:4 * top]
+    all_w_f = all_route_f / jnp.sum(all_route_f, axis=-1, keepdims=True)
+    all_w_b = all_route_b / jnp.sum(all_route_b, axis=-1, keepdims=True)
     all_h_f = gather(h_f)
-    all_ids_f = gather(ids_fwd[0])
-    all_w_f = gather(weights_f)
     all_h_b = gather(h_b)
     all_g = gather(grad)
-    all_ids_b = gather(ids_bwd[0])
-    all_w_b = gather(weights_b)
 
     onehot_f, _ = expert_slots(all_ids_f, all_w_f, me, cap)
     rows = pick_rows(onehot_f, all_h_f).reshape(-1, width)

time: 462 us -> 462 us (level)
  blocking collectives: 77.6 us -> 26 us
  waiting for transfers between devices: 277 us -> 328 us
    all_gather x3 -> x1, blocking collectives: 77.6 us -> 26 us  [gather(): return lax.all_gather(v, 'ep', axis=0, tiled=False)]
    all_gather x3, waiting for transfers between devices: 140 us -> 192 us  [gather(): return lax.all_gather(v, 'ep', axis=0, tiled=False)]
where the time goes in v2:
time: 462 us; the launch traced here: 461 us
  waiting for transfers between devices  328 us (71%)
  matrix products  62.8 us (14%)
  blocking collectives  26 us (6%)
  between operations  14 us (3%)
  starting transfers between devices  13.3 us (3%)
  other arithmetic  10 us (2%)
  local copies, waits for them, and re-layouts  7.04 us (2%)
    all_gather x3, waiting for transfers between devices, gather(): return lax.all_gather(v, 'ep', axis=0, tiled=False)  192 us
    all_to_all x1, waiting for transfers between devices, local(): lax.all_to_all(made_b, 'ep', split_axis=0, concat_axis=0, tiled=True)  68.5 us
    all_to_all x1, waiting for transfers between devices, local(): lax.all_to_all(made_f, 'ep', split_axis=0, concat_axis=0, tiled=True)  66.2 us
    all_gather x1, blocking collectives, gather(): return lax.all_gather(v, 'ep', axis=0, tiled=False)  26 us
    dot_general x1, matrix products, expert_backward(): jnp.dot(dgate, w_g.T, preferred_element_type=jnp.float32)  12.7 us
    dot_general x1, matrix products, expert_forward(): jnp.dot(act, w_d, preferred_element_type=jnp.float32).astype(jnp.bfloat16)  11.9 us
    dot_general x3, matrix products, pick_rows(): jnp.einsum('bct,btd->bcd', onehot, rows, preferred_element_type=jnp.float32)  9.72 us
  transfers between devices with their start and end apart: 7, of which 6 were waited for; matrix products, arithmetic and copies ran while one was open for 5% of the time, Pallas kernels for 0%

profile of v2, /device:TPU:13, one launch (start us, length us, event | category | flops | bytes accessed | tf_op | source)
XLA Modules:
  0.0 461.2 jit_solution(16096429252175732777)
XLA Ops:
  7.2 0.0 copy-start
  7.2 0.0 all-gather.8.cloned.1.call-start
  7.2 0.7 all-gather.8.cloned.1.call-update
  7.9 0.0 all-gather.10.cloned.1.call-start
  8.0 0.9 mul.219
  8.8 1.1 fusion.34
  9.9 1.8 fusion.41
  11.7 0.0 all-gather.10.cloned.1.call-update
  11.8 0.7 convert_bitcast_fusion.1
  12.5 0.7 maximum_bitcast_fusion
  13.2 26.0 %all-gather.1 = f32[16,64,32]{1,2,0:T(8,128)S(1)} all-gather(f32[1,64,32]{1,2,0:T(8,128)S(1)} %maximum_bitcast_fusion), channel_id=2, replica_groups=mesh['pipe'=2,'ep'=16] {'ep'}, dimensions={0}, use_global_device_ids=true | all-gather | bytes 139264 | tf_op jit(solution)/shard_map/all_gather | solution.py:100
  39.2 0.1 fusion.73
  39.3 0.2 reduce_window_sum.47
  39.5 0.2 select_reduce_fusion
  39.7 47.6 %all-gather.8.cloned.1.call-done = bf16[16,64,2048]{2,1,0:T(8,128)(2,1)} async-done(((bf16[1,64,2048]{2,1,0:T(8,128)(2,1)}), bf16[16,64,2048]{2,1,0:T(8,128)(2,1)}) %all-gather.8.cloned.1.call-update) | async-done | bytes 4194320 | tf_op jit(solution)/shard_map/all_gather | solution.py:100
  87.3 3.3 multiply_convert_fusion
  90.6 4.0 fusion.1
  94.7 70.2 %all-gather.10.cloned.1.call-done = bf16[16,64,2048]{2,1,0:T(8,128)(2,1)} async-done(((bf16[1,64,2048]{2,1,0:T(8,128)(2,1)}), bf16[16,64,2048]{2,1,0:T(8,128)(2,1)}) %all-gather.10.cloned.1.call-update) | async-done | bytes 4194320 | tf_op jit(solution)/shard_map/all_gather | solution.py:100
  164.9 3.3 convolution_convert_fusion
  168.2 0.0 copy-start.2
  168.2 1.7 copy-done.2
  169.9 0.0 copy-done.10
  169.9 4.1 fusion.11
  174.0 12.7 %fusion.9 = f32[768,2048]{1,0:T(8,128)} fusion(bf16[1,1,2048,768]{3,2,1,0:T(8,128)(2,1)} %param.19, f32[768,768]{1,0:T(8,128)} %fusion.11, f32[768,768]{1,0:T(8,128)} %fusion.1, bf16[768,2048]{1,0:T(8,128)(2,1)} %bitcast.125, bf16[1,1,2048,768]{3,2,1,0:T(8,128)(2,1)S(1)} %copy-done), kind=kOutput, calls=%fused_computation.16 | convolution fusion | flops 4837736448 | bytes 20447232 | tf_op jit(solution)/shard_map/dot_general | solution.py:43
  186.7 7.4 %add_convert_fusion = bf16[768,2048]{1,0:T(8,128)(2,1)} fusion(f32[768,2048]{1,0:T(8,128)} %fusion.9, bf16[1,1,2048,768]{3,2,1,0:T(8,128)(2,1)S(1)} %copy-done, f32[768,768]{1,0:T(8,128)} %fusion.1, f32[768,768]{1,0:T(8,128)} %fusion.11), kind=kOutput, calls=%fused_computation.1 | convolution fusion | flops 2422603776 | bytes 17301504 | tf_op jit(solution)/shard_map/dot_general | solution.py:43
  194.2 4.7 %all-to-all-start.1 = ((bf16[16,48,2048]{2,1,0:T(8,128)(2,1)}), bf16[16,48,2048]{2,1,0:T(8,128)(2,1)}, u32[]{:S(2)}, u32[]{:S(2)}) async-start(bf16[16,48,2048]{2,1,0:T(8,128)(2,1)} %bitcast.129), calls=%async_computation.1 | async-start | bytes 6291456 | tf_op jit(solution)/shard_map/all_to_all | solution.py:128
  198.9 0.0 all-gather.6.cloned.1.call-start
  198.9 0.1 copy.30
  199.0 0.1 eq.165
  199.1 0.1 eq.161
  199.2 1.2 reduce-window.16
  200.4 0.2 slice_reduce_fusion.1
  200.6 0.1 fusion.64
  200.7 0.1 reduce_sum.115
  200.8 0.2 fusion.36
  201.0 68.5 %all-to-all-done.1 = bf16[16,48,2048]{2,1,0:T(8,128)(2,1)} async-done(((bf16[16,48,2048]{2,1,0:T(8,128)(2,1)}), bf16[16,48,2048]{2,1,0:T(8,128)(2,1)}, u32[]{:S(2)}, u32[]{:S(2)}) %all-to-all-start.1) | async-done | bytes 3145760 | tf_op jit(solution)/shard_map/all_to_all | solution.py:128
  269.5 4.3 convolution_reduce_fusion
  273.8 0.2 fusion.35
  274.0 1.1 fusion.45
  275.1 0.0 all-gather.6.cloned.1.call-update
  275.1 0.2 reduce_window_sum.44
  275.3 73.8 %all-gather.6.cloned.1.call-done = bf16[16,64,2048]{2,1,0:T(8,128)(2,1)} async-done(((bf16[1,64,2048]{2,1,0:T(8,128)(2,1)}), bf16[16,64,2048]{2,1,0:T(8,128)(2,1)}) %all-gather.6.cloned.1.call-update) | async-done | bytes 4194320 | tf_op jit(solution)/shard_map/all_gather | solution.py:100
  349.1 3.1 convolution_convert_fusion.3
  352.3 1.7 copy-done.3
  354.0 4.0 fusion.7
  358.0 11.9 %convolution_convert_fusion.2 = bf16[768,2048]{1,0:T(8,128)(2,1)} fusion(bf16[1,1,768,2048]{3,2,1,0:T(8,128)(2,1)} %param.21, f32[768,768]{1,0:T(8,128)} %fusion.7, bf16[768,2048]{1,0:T(8,128)(2,1)} %bitcast.127, bf16[1,1,2048,768]{3,2,1,0:T(8,128)(2,1)} %param.19), kind=kOutput, calls=%fused_computation.6 | convolution fusion | flops 4836950016 | bytes 14942208 | tf_op jit(solution)/shard_map/dot_general | solution.py:33
  369.9 4.7 %all-to-all-start = ((bf16[16,48,2048]{2,1,0:T(8,128)(2,1)}), bf16[16,48,2048]{2,1,0:T(8,128)(2,1)}, u32[]{:S(2)}, u32[]{:S(2)}) async-start(bf16[16,48,2048]{2,1,0:T(8,128)(2,1)} %bitcast.128), calls=%async_computation | async-start | bytes 6291456 | tf_op jit(solution)/shard_map/all_to_all | solution.py:121
  374.7 0.1 copy.26
  374.7 0.1 eq.148
  374.8 0.1 eq.144
  374.9 1.2 reduce-window.14
  376.1 0.2 slice_reduce_fusion.2
  376.3 0.1 fusion.67
  376.4 0.1 reduce_sum.109
  376.6 0.1 copy.25
  376.7 2.3 collective-permute-start.1
  379.0 66.2 %all-to-all-done = bf16[16,48,2048]{2,1,0:T(8,128)(2,1)} async-done(((bf16[16,48,2048]{2,1,0:T(8,128)(2,1)}), bf16[16,48,2048]{2,1,0:T(8,128)(2,1)}, u32[]{:S(2)}, u32[]{:S(2)}) %all-to-all-start) | async-done | bytes 3145760 | tf_op jit(solution)/shard_map/all_to_all | solution.py:121
  445.2 4.4 multiply_reduce_fusion
  449.6 0.1 fusion.39
  449.7 1.5 collective-permute-start
  451.2 0.0 collective-permute-done.1
  451.2 1.2 collective-permute-done
  452.3 0.7 copy.40
  453.0 1.7 copy.41
  (35 shorter events, 0.3 us)
Async XLA Ops:
  7.2 166.8 %copy-start = (bf16[1,1,2048,768]{3,2,1,0:T(8,128)(2,1)S(1)}, bf16[1,1,2048,768]{3,2,1,0:T(8,128)(2,1)}, u32[]{:S(2)}) copy-start(bf16[1,1,2048,768]{3,2,1,0:T(8,128)(2,1)} %param.20) | copy-start | bytes 9437188
  7.2 80.1 %all-gather.8.cloned.1.call-start = ((), (), s32[]{:S(2)}) async-start(), calls=%async_computation.3 | async-start | bytes 4456448 | tf_op jit(solution)/shard_map/all_gather | solution.py:100
  7.9 157.0 %all-gather.10.cloned.1.call-start = ((), (), s32[]{:S(2)}) async-start(), calls=%async_computation.4 | async-start | bytes 4456448 | tf_op jit(solution)/shard_map/all_gather | solution.py:100
  87.3 3.3 copy-start.9
  164.9 5.0 %copy-start.10 = (bf16[1,1,2048,768]{3,2,1,0:T(8,128)(2,1)S(1)}, bf16[1,1,2048,768]{3,2,1,0:T(8,128)(2,1)}, u32[]{:S(2)}) copy-start(bf16[1,1,2048,768]{3,2,1,0:T(8,128)(2,1)} %param.19) | copy-start | bytes 9437188
  168.2 1.7 copy-start.2
  194.2 4.7 %copy-start.7 = (s32[1,64,8]{1,2,0:T(8,128)S(1)}, s32[1,64,8]{1,2,0:T(8,128)}, u32[]{:S(2)}) copy-start(s32[1,64,8]{1,2,0:T(8,128)} %param.16) | copy-start | bytes 6148
  194.2 6.6 %copy-start.4 = (bf16[1,64,2048]{2,1,0:T(8,128)(2,1)S(1)}, bf16[1,64,2048]{2,1,0:T(8,128)(2,1)}, u32[]{:S(2)}) copy-start(bf16[1,64,2048]{2,1,0:T(8,128)(2,1)} %param.11) | copy-start | bytes 786436
  194.2 75.3 %all-to-all-start.1 = ((bf16[16,48,2048]{2,1,0:T(8,128)(2,1)}), bf16[16,48,2048]{2,1,0:T(8,128)(2,1)}, u32[]{:S(2)}, u32[]{:S(2)}) async-start(bf16[16,48,2048]{2,1,0:T(8,128)(2,1)} %bitcast.129), calls=%async_computation.1 | async-start | bytes 6291456 | tf_op jit(solution)/shard_map/all_to_all | solution.py:128
  198.9 150.3 %all-gather.6.cloned.1.call-start = ((), (), s32[]{:S(2)}) async-start(), calls=%async_computation.2 | async-start | bytes 4456448 | tf_op jit(solution)/shard_map/all_gather | solution.py:100
  269.5 4.4 copy-start.1
  269.5 4.6 copy-start.5
  352.3 1.7 copy-start.3
  369.9 4.7 %copy-start.8 = (s32[1,64,8]{1,2,0:T(8,128)S(1)}, s32[1,64,8]{1,2,0:T(8,128)}, u32[]{:S(2)}) copy-start(s32[1,64,8]{1,2,0:T(8,128)} %param.12) | copy-start | bytes 6148
  369.9 6.6 %copy-start.6 = (f32[1,64,8]{1,2,0:T(8,128)S(1)}, f32[1,64,8]{1,2,0:T(8,128)}, u32[]{:S(2)}) copy-start(f32[1,64,8]{1,2,0:T(8,128)} %param.13) | copy-start | bytes 6148
  369.9 75.3 %all-to-all-start = ((bf16[16,48,2048]{2,1,0:T(8,128)(2,1)}), bf16[16,48,2048]{2,1,0:T(8,128)(2,1)}, u32[]{:S(2)}, u32[]{:S(2)}) async-start(bf16[16,48,2048]{2,1,0:T(8,128)(2,1)} %bitcast.128), calls=%async_computation | async-start | bytes 6291456 | tf_op jit(solution)/shard_map/all_to_all | solution.py:121
  376.7 74.5 %collective-permute-start.1 = (bf16[1,64,2048]{2,1,0:T(8,128)(2,1)}, bf16[1,64,2048]{2,1,0:T(8,128)(2,1)}, u32[]{:S(2)}, u32[]{:S(2)}) collective-permute-start(bf16[1,64,2048]{2,1,0:T(8,128)(2,1)} %get-tuple-element.5), channel_id=1, source_target_pairs={{16,0},{0,16},{17,1},{1,17},{18,2},{2,18},{19,3},{3,19},{20,4},{4,... | collective-permute-start | bytes 786440 | tf_op jit(solution)/shard_map/ppermute | solution.py:12
  449.7 2.6 collective-permute-start
Sparse Core Ops, SparseCore 0:
  10.8 76.5 all-gather.7
  90.6 74.1 all-gather.9
  275.2 73.8 all-gather.5

commit v3 on v2

--- a/solution.py
+++ b/solution.py
@@ -73,6 +73,47 @@
     onehot = (places[:, None] == jnp.arange(count, dtype=jnp.int32)[None, :]).astype(jnp.bfloat16)
     picked = jnp.dot(onehot, back, preferred_element_type=jnp.float32)
     return picked.reshape(-1, top, back.shape[1])
+
+
+def _pairs(n, n2, stage, move):
+    out = []
+    for i in range(n):
+        e1, e2 = i // n2, i % n2
+        if stage == 1:
+            e1 = move(e1)
+        else:
+            e2 = move(e2)
+        out.append((i, e1 * n2 + e2))
+    return out
+
+
+def gather_ep(v, axis_name):
+    n = lax.axis_size(axis_name)
+    n2 = 4
+    if n % n2 or v.shape[0] % 2:
+        return lax.all_gather(v, axis_name, axis=0, tiled=False)
+    n1 = n // n2
+    me = lax.axis_index(axis_name)
+    e1, e2 = me // n2, me % n2
+    s1 = jnp.zeros((n1,) + v.shape, v.dtype)
+    s1 = lax.dynamic_update_index_in_dim(s1, v, e1, 0)
+    for d in range(1, n1):
+        got = lax.ppermute(v, axis_name, _pairs(n, n2, 1, lambda a: (a + d) % n1))
+        s1 = lax.dynamic_update_index_in_dim(s1, got, (e1 - d) % n1, 0)
+    flip_x = lambda a: a ^ 1
+    flip_y = lambda a: a ^ 2
+    px = lax.ppermute(s1, axis_name, _pairs(n, n2, 2, flip_x))
+    py = lax.ppermute(s1, axis_name, _pairs(n, n2, 2, flip_y))
+    h = v.shape[0] // 2
+    d1 = lax.ppermute(px[:, :h], axis_name, _pairs(n, n2, 2, flip_y))
+    d2 = lax.ppermute(py[:, h:], axis_name, _pairs(n, n2, 2, flip_x))
+    diag = jnp.concatenate([d1, d2], axis=1)
+    s2 = jnp.zeros((n2,) + s1.shape, v.dtype)
+    s2 = lax.dynamic_update_index_in_dim(s2, s1, e2, 0)
+    s2 = lax.dynamic_update_index_in_dim(s2, px, e2 ^ 1, 0)
+    s2 = lax.dynamic_update_index_in_dim(s2, py, e2 ^ 2, 0)
+    s2 = lax.dynamic_update_index_in_dim(s2, diag, e2 ^ 3, 0)
+    return jnp.swapaxes(s2, 0, 1).reshape((n,) + v.shape)
 
 
 def local(
@@ -97,7 +138,7 @@
     weights_b = route_bwd[0] / jnp.sum(route_bwd[0], axis=-1, keepdims=True)
 
     def gather(v):
-        return lax.all_gather(v, "ep", axis=0, tiled=False)
+        return gather_ep(v, "ep")
 
     tables = gather(
         jnp.concatenate(
@@ -112,8 +153,9 @@
     all_w_f = all_route_f / jnp.sum(all_route_f, axis=-1, keepdims=True)
     all_w_b = all_route_b / jnp.sum(all_route_b, axis=-1, keepdims=True)
     all_h_f = gather(h_f)
-    all_h_b = gather(h_b)
-    all_g = gather(grad)
+    both_b = gather(jnp.concatenate([h_b, grad], axis=-1))
+    all_h_b = both_b[..., :width]
+    all_g = both_b[..., width:]
 
     onehot_f, _ = expert_slots(all_ids_f, all_w_f, me, cap)
     rows = pick_rows(onehot_f, all_h_f).reshape(-1, width)

time: 462 us -> 412 us (0.89)
  waiting for transfers between devices: 328 us -> 276 us
  blocking collectives: 26 us -> 0 us
  local copies, waits for them, and re-layouts: 7.04 us -> 32.7 us
  starting transfers between devices: 13.3 us -> 27.5 us
  between operations: 14 us -> 1.22 us
  other arithmetic: 10 us -> 17 us
  matrix products: 62.8 us -> 56.2 us
    all_gather x3 -> x0, waiting for transfers between devices: 192 us -> none  [gather(): return lax.all_gather(v, 'ep', axis=0, tiled=False)]
    ppermute x0 -> x21, waiting for transfers between devices: none -> 144 us  [the longest x3 63.5 us: gather_ep(): px = lax.ppermute(s1, axis_name, _pairs(n, n2, 2, flip_x))]
    all_gather x1 -> x0, blocking collectives: 26 us -> none  [gather(): return lax.all_gather(v, 'ep', axis=0, tiled=False)]
    dynamic_update_slice x0 -> x18, local copies, waits for them, and re-layouts: none -> 17.1 us  [the longest x9 7.53 us: gather_ep(): s1 = lax.dynamic_update_index_in_dim(s1, got, (e1 - d) % n1, 0)]
    ppermute x0 -> x21, starting transfers between devices: none -> 13.9 us  [the longest x9 8.47 us: gather_ep(): got = lax.ppermute(v, axis_name, _pairs(n, n2, 1, lambda a: (a + d) % n1))]
    dot_general x3, matrix products: 9.72 us -> 2.91 us  [pick_rows(): jnp.einsum('bct,btd->bcd', onehot, rows, preferred_element_type=jnp.float32)]
    slice x1 -> x6, local copies, waits for them, and re-layouts: 0.22 us -> 5.04 us  [the longest x3 2.45 us: gather_ep(): d2 = lax.ppermute(py[:, h:], axis_name, _pairs(n, n2, 2, flip_x))]
  transfers between devices with their start and end apart: 7 -> 25, of which waited for: 6 -> 15; matrix products, arithmetic and copies ran while one was open for 5% -> 11% of each run, Pallas kernels for 0% -> 0%
where the time goes in v3:
time: 412 us; the launch traced here: 410 us
  waiting for transfers between devices  276 us (67%)
  matrix products  56.2 us (14%)
  local copies, waits for them, and re-layouts  32.7 us (8%)
  starting transfers between devices  27.5 us (7%)
  other arithmetic  17 us (4%)
    all_to_all x1, waiting for transfers between devices, local(): lax.all_to_all(made_b, 'ep', split_axis=0, concat_axis=0, tiled=True)  68.7 us
    ppermute x3, waiting for transfers between devices, gather_ep(): px = lax.ppermute(s1, axis_name, _pairs(n, n2, 2, flip_x))  63.5 us
    all_to_all x1, waiting for transfers between devices, local(): lax.all_to_all(made_f, 'ep', split_axis=0, concat_axis=0, tiled=True)  61.9 us
    ppermute x9, waiting for transfers between devices, gather_ep(): got = lax.ppermute(v, axis_name, _pairs(n, n2, 1, lambda a: (a + d) % n1))  50.5 us
    ppermute x3, waiting for transfers between devices, gather_ep(): d1 = lax.ppermute(px[:, :h], axis_name, _pairs(n, n2, 2, flip_y))  24.5 us
    dot_general x1, matrix products, expert_backward(): jnp.dot(dgate, w_g.T, preferred_element_type=jnp.float32)  12.9 us
    dot_general x1, matrix products, expert_forward(): jnp.dot(act, w_d, preferred_element_type=jnp.float32).astype(jnp.bfloat16)  11.9 us
    dot_general x2, matrix products, combine_rows(): picked = jnp.dot(onehot, back, preferred_element_type=jnp.float32)  8.81 us
  transfers between devices with their start and end apart: 25, of which 15 were waited for; matrix products, arithmetic and copies ran while one was open for 11% of the time, Pallas kernels for 0%

profile of v3, /device:TPU:13, one launch (start us, length us, event | category | flops | bytes accessed | tf_op | source)
XLA Modules:
  0.0 410.5 jit_solution(11476752101015523907)
XLA Ops:
  0.7 0.9 convert_bitcast_fusion.2
  2.4 1.3 collective-permute-start
  3.6 1.1 collective-permute-start.1
  4.7 1.4 collective-permute-start.2
  6.8 1.1 fusion.51
  8.5 1.1 fusion.53
  9.6 1.8 pad_maximum_fusion
  11.4 3.1 collective-permute-start.16
  14.5 1.6 broadcast_in_dim.158
  16.1 1.8 bitcast_dynamic-update-slice_fusion.9
  18.8 1.3 collective-permute-start.3
  20.4 3.2 collective-permute-done.4
  24.2 1.9 bitcast_dynamic-update-slice_fusion.8
  26.1 29.2 %collective-permute-done.16 = bf16[64,4096]{1,0:T(8,128)(2,1)} collective-permute-done((bf16[64,4096]{1,0:T(8,128)(2,1)}, bf16[64,4096]{1,0:T(8,128)(2,1)}, u32[]{:S(2)}, u32[]{:S(2)}) %collective-permute-start.16) | collective-permute-done | bytes 524320 | tf_op jit(solution)/shard_map/ppermute | solution.py:101
  55.3 1.9 bitcast_dynamic-update-slice_fusion.7
  57.2 2.6 collective-permute-done.17
  59.8 0.8 bitcast_dynamic-update-slice_fusion.6
  60.7 1.2 collective-permute-start.18
  62.8 1.0 broadcast_in_dim.157
  63.8 1.9 bitcast_dynamic-update-slice_fusion.2
  65.7 41.5 %collective-permute-done.18 = bf16[4,64,4096]{2,1,0:T(8,128)(2,1)} collective-permute-done((bf16[4,64,4096]{2,1,0:T(8,128)(2,1)}, bf16[4,64,4096]{2,1,0:T(8,128)(2,1)}, u32[]{:S(2)}, u32[]{:S(2)}) %collective-permute-start.18) | collective-permute-done | bytes 2097184 | tf_op jit(solution)/shard_map/ppermute | solution.py:105
  107.2 1.3 slice.69
  108.8 1.3 slice.70
  110.1 1.3 collective-permute-start.21
  111.3 1.8 bitcast_dynamic-update-slice_fusion.1
  113.2 1.9 bitcast_dynamic-update-slice_fusion
  115.1 16.3 %collective-permute-done.20 = bf16[4,32,4096]{2,1,0:T(8,128)(2,1)S(1)} collective-permute-done((bf16[4,32,4096]{2,1,0:T(8,128)(2,1)S(1)}, bf16[4,32,4096]{2,1,0:T(8,128)(2,1)S(1)}, u32[]{:S(2)}, u32[]{:S(2)}) %collective-permute-start.20) | collective-permute-done | bytes 1048608 | tf_op jit(solution)/shard_map/ppermute | solution.py:108
  131.4 1.3 collective-permute-done.21
  133.0 1.0 fusion.8
  134.0 1.0 multiply_convert_fusion
  135.0 2.0 copy-done.13
  137.0 4.1 %fusion.11 = f32[768,768]{1,0:T(8,128)} fusion(bf16[768,2048]{1,0:T(8,128)(2,1)S(1)} %bitcast.224, bf16[1,1,768,2048]{3,2,1,0:T(8,128)(2,1)S(1)} %copy-done.13), kind=kOutput, calls=%fused_computation.12 | convolution fusion | flops 2415919104 | bytes 8650752 | tf_op jit(solution)/shard_map/dot_general | solution.py:40
  141.2 4.0 fusion.21
  145.2 12.9 %fusion.19 = f32[768,2048]{1,0:T(8,128)} fusion(bf16[1,1,2048,768]{3,2,1,0:T(8,128)(2,1)} %param.19, f32[768,768]{1,0:T(8,128)} %fusion.21, f32[768,768]{1,0:T(8,128)} %fusion.11, bf16[768,2048]{1,0:T(8,128)(2,1)} %bitcast.219, bf16[1,1,2048,768]{3,2,1,0:T(8,128)(2,1)S(1)} %copy-done), kind=kOutput, calls=%fused_computation.20 | convolution fusion | flops 4837736448 | bytes 20447232 | tf_op jit(solution)/shard_map/dot_general | solution.py:43
  158.1 7.5 %add_convert_fusion = bf16[768,2048]{1,0:T(8,128)(2,1)} fusion(f32[768,2048]{1,0:T(8,128)} %fusion.19, bf16[1,1,2048,768]{3,2,1,0:T(8,128)(2,1)S(1)} %copy-done, f32[768,768]{1,0:T(8,128)} %fusion.11, f32[768,768]{1,0:T(8,128)} %fusion.21), kind=kOutput, calls=%fused_computation.1 | convolution fusion | flops 2422603776 | bytes 17301504 | tf_op jit(solution)/shard_map/dot_general | solution.py:43
  165.6 4.8 %all-to-all-start.1 = ((bf16[16,48,2048]{2,1,0:T(8,128)(2,1)}), bf16[16,48,2048]{2,1,0:T(8,128)(2,1)}, u32[]{:S(2)}, u32[]{:S(2)}) async-start(bf16[16,48,2048]{2,1,0:T(8,128)(2,1)} %bitcast.223), calls=%async_computation.1 | async-start | bytes 6291456 | tf_op jit(solution)/shard_map/all_to_all | solution.py:170
  170.6 1.2 reduce-window.16
  172.4 68.7 %all-to-all-done.1 = bf16[16,48,2048]{2,1,0:T(8,128)(2,1)} async-done(((bf16[16,48,2048]{2,1,0:T(8,128)(2,1)}), bf16[16,48,2048]{2,1,0:T(8,128)(2,1)}, u32[]{:S(2)}, u32[]{:S(2)}) %all-to-all-start.1) | async-done | bytes 3145760 | tf_op jit(solution)/shard_map/all_to_all | solution.py:170
  241.1 4.3 %convolution_reduce_fusion = f32[64,2048]{1,0:T(8,128)S(1)} fusion(bf16[768,2048,1]{1,0,2:T(8,128)(2,1)} %bitcast.64, s32[64,8]{1,0:T(8,128)S(1)} %bitcast_add_fusion), kind=kOutput, calls=%fused_computation.35 | convolution fusion | flops 1611923456 | bytes 3672064 | tf_op jit(solution)/shard_map/dot_general | solution.py:74
  246.2 1.1 broadcast_in_dim.146
  248.1 1.5 collective-permute-start.9
  249.6 3.0 collective-permute-done.7
  253.4 14.2 %collective-permute-done.8 = bf16[64,2048]{1,0:T(8,128)(2,1)S(1)} collective-permute-done((bf16[64,2048]{1,0:T(8,128)(2,1)S(1)}, bf16[64,2048]{1,0:T(8,128)(2,1)S(1)}, u32[]{:S(2)}, u32[]{:S(2)}) %collective-permute-start.8) | collective-permute-done | bytes 262176 | tf_op jit(solution)/shard_map/ppermute | solution.py:101
  268.3 1.4 collective-permute-done.9
  271.5 1.3 bitcast_dynamic-update-slice_fusion.5
  272.8 22.0 %collective-permute-done.10 = bf16[4,64,2048]{2,1,0:T(8,128)(2,1)} collective-permute-done((bf16[4,64,2048]{2,1,0:T(8,128)(2,1)}, bf16[4,64,2048]{2,1,0:T(8,128)(2,1)}, u32[]{:S(2)}, u32[]{:S(2)}) %collective-permute-start.10) | collective-permute-done | bytes 1048608 | tf_op jit(solution)/shard_map/ppermute | solution.py:105
  294.9 1.1 slice.64
  296.0 1.1 slice.65
  297.2 1.3 bitcast_dynamic-update-slice_fusion.3
  298.5 1.3 bitcast_dynamic-update-slice_fusion.4
  299.9 8.1 %collective-permute-done.12 = bf16[4,32,2048]{2,1,0:T(8,128)(2,1)S(1)} collective-permute-done((bf16[4,32,2048]{2,1,0:T(8,128)(2,1)S(1)}, bf16[4,32,2048]{2,1,0:T(8,128)(2,1)S(1)}, u32[]{:S(2)}, u32[]{:S(2)}) %collective-permute-start.12) | collective-permute-done | bytes 524320 | tf_op jit(solution)/shard_map/ppermute | solution.py:108
  308.0 1.2 collective-permute-done.13
  309.3 1.0 convolution_convert_fusion.1
  310.3 1.7 copy-done.6
  312.0 4.0 fusion.17
  316.0 11.9 %convolution_convert_fusion = bf16[768,2048]{1,0:T(8,128)(2,1)} fusion(bf16[1,1,768,2048]{3,2,1,0:T(8,128)(2,1)} %param.21, f32[768,768]{1,0:T(8,128)} %fusion.17, bf16[768,2048]{1,0:T(8,128)(2,1)} %bitcast.221, bf16[1,1,2048,768]{3,2,1,0:T(8,128)(2,1)} %param.19), kind=kOutput, calls=%fused_computation.10 | convolution fusion | flops 4836950016 | bytes 14942208 | tf_op jit(solution)/shard_map/dot_general | solution.py:33
  327.9 4.7 %all-to-all-start = ((bf16[16,48,2048]{2,1,0:T(8,128)(2,1)}), bf16[16,48,2048]{2,1,0:T(8,128)(2,1)}, u32[]{:S(2)}, u32[]{:S(2)}) async-start(bf16[16,48,2048]{2,1,0:T(8,128)(2,1)} %bitcast.222), calls=%async_computation | async-start | bytes 6291456 | tf_op jit(solution)/shard_map/all_to_all | solution.py:163
  332.9 1.2 reduce-window.14
  335.3 2.0 fusion.58
  337.4 2.6 collective-permute-start.22
  340.0 61.9 %all-to-all-done = bf16[16,48,2048]{2,1,0:T(8,128)(2,1)} async-done(((bf16[16,48,2048]{2,1,0:T(8,128)(2,1)}), bf16[16,48,2048]{2,1,0:T(8,128)(2,1)}, u32[]{:S(2)}, u32[]{:S(2)}) %all-to-all-start) | async-done | bytes 3145760 | tf_op jit(solution)/shard_map/all_to_all | solution.py:163
  401.9 4.5 %multiply_reduce_fusion = f32[64,2048]{1,0:T(8,128)S(1)} fusion(bf16[768,2048,1]{1,0,2:T(8,128)(2,1)} %bitcast.38, f32[64,8]{1,0:T(8,128)S(1)} %copy.20, s32[64,8]{1,0:T(8,128)S(1)} %bitcast_add_fusion.1), kind=kOutput, calls=%fused_computation.7 | convolution fusion | flops 1612972032 | bytes 3674112 | tf_op jit(solution)/shard_map/dot_general | solution.py:74
  406.4 1.5 collective-permute-start.14
  407.9 1.2 collective-permute-done.14
  (111 shorter events, 14.2 us)
Async XLA Ops:
  0.6 144.5 %copy-start = (bf16[1,1,2048,768]{3,2,1,0:T(8,128)(2,1)S(1)}, bf16[1,1,2048,768]{3,2,1,0:T(8,128)(2,1)}, u32[]{:S(2)}) copy-start(bf16[1,1,2048,768]{3,2,1,0:T(8,128)(2,1)} %param.20) | copy-start | bytes 9437188
  0.6 17.2 %copy-start.8 = (f32[1,64,8]{1,2,0:T(8,128)S(1)}, f32[1,64,8]{1,2,0:T(8,128)}, u32[]{:S(2)}) copy-start(f32[1,64,8]{1,2,0:T(8,128)} %param.13) | copy-start | bytes 6148
  0.7 17.2 %copy-start.11 = (f32[1,64,8]{1,2,0:T(8,128)S(1)}, f32[1,64,8]{1,2,0:T(8,128)}, u32[]{:S(2)}) copy-start(f32[1,64,8]{1,2,0:T(8,128)} %param.17) | copy-start | bytes 6148
  2.4 15.6 %collective-permute-start = (f32[64,32]{0,1:T(8,128)S(1)}, f32[64,32]{0,1:T(8,128)}, u32[]{:S(2)}, u32[]{:S(2)}) collective-permute-start(f32[64,32]{0,1:T(8,128)S(1)} %pad_maximum_fusion.1), channel_id=1, source_target_pairs={{0,4},{1,5},{2,6},{3,7},{4,8},{5,9},{6,10},{7,11},{8,12},{9,13},{1... | collective-permute-start | bytes 24584 | tf_op jit(solution)/shard_map/ppermute | solution.py:101
  3.6 15.1 %collective-permute-start.1 = (f32[64,32]{0,1:T(8,128)S(1)}, f32[64,32]{0,1:T(8,128)S(1)}, u32[]{:S(2)}, u32[]{:S(2)}) collective-permute-start(f32[64,32]{0,1:T(8,128)S(1)} %pad_maximum_fusion.1), channel_id=1, source_target_pairs={{0,8},{1,9},{2,10},{3,11},{4,12},{5,13},{6,14},{7,15},{8,0},{9,1},... | collective-permute-start | bytes 24584 | tf_op jit(solution)/shard_map/ppermute | solution.py:101
  4.7 14.1 %collective-permute-start.2 = (f32[64,32]{0,1:T(8,128)S(1)}, f32[64,32]{0,1:T(8,128)S(1)}, u32[]{:S(2)}, u32[]{:S(2)}) collective-permute-start(f32[64,32]{0,1:T(8,128)S(1)} %pad_maximum_fusion.1), channel_id=1, source_target_pairs={{0,12},{1,13},{2,14},{3,15},{4,0},{5,1},{6,2},{7,3},{8,4},{9,5},{1... | collective-permute-start | bytes 24584 | tf_op jit(solution)/shard_map/ppermute | solution.py:101
  11.3 12.9 %collective-permute-start.15 = (bf16[64,4096]{1,0:T(8,128)(2,1)}, bf16[64,4096]{1,0:T(8,128)(2,1)}, u32[]{:S(2)}, u32[]{:S(2)}) collective-permute-start(bf16[64,4096]{1,0:T(8,128)(2,1)} %pad_maximum_fusion), channel_id=1, source_target_pairs={{0,4},{1,5},{2,6},{3,7},{4,8},{5,9},{6,10},{7,11},{8,12},{9,13},{1... | collective-permute-start | bytes 1572872 | tf_op jit(solution)/shard_map/ppermute | solution.py:101
  11.4 43.9 %collective-permute-start.16 = (bf16[64,4096]{1,0:T(8,128)(2,1)}, bf16[64,4096]{1,0:T(8,128)(2,1)}, u32[]{:S(2)}, u32[]{:S(2)}) collective-permute-start(bf16[64,4096]{1,0:T(8,128)(2,1)} %pad_maximum_fusion), channel_id=1, source_target_pairs={{0,8},{1,9},{2,10},{3,11},{4,12},{5,13},{6,14},{7,15},{8,0},{9,1},... | collective-permute-start | bytes 1572872 | tf_op jit(solution)/shard_map/ppermute | solution.py:101
  18.0 41.8 %collective-permute-start.17 = (bf16[64,4096]{1,0:T(8,128)(2,1)}, bf16[64,4096]{1,0:T(8,128)(2,1)S(1)}, u32[]{:S(2)}, u32[]{:S(2)}) collective-permute-start(bf16[64,4096]{1,0:T(8,128)(2,1)} %pad_maximum_fusion), channel_id=1, source_target_pairs={{0,12},{1,13},{2,14},{3,15},{4,0},{5,1},{6,2},{7,3},{8,4},{9,5},{1... | collective-permute-start | bytes 1572872 | tf_op jit(solution)/shard_map/ppermute | solution.py:101
  18.8 5.2 %collective-permute-start.3 = (f32[4,64,32]{1,2,0:T(8,128)S(1)}, f32[4,64,32]{1,2,0:T(8,128)S(1)}, u32[]{:S(2)}, u32[]{:S(2)}) collective-permute-start(f32[4,64,32]{1,2,0:T(8,128)S(1)} %bitcast_dynamic-update-slice_fusion.16), channel_id=1, source_target_pairs={{0,1},{1,0},{2,3},{3,2},{4,5},{5,4},{6,7},{7,6},{8,9},{9,8},{10,11... | collective-permute-start | bytes 98312 | tf_op jit(solution)/shard_map/ppermute | solution.py:105
  20.1 3.5 collective-permute-start.4
  23.7 38.4 %collective-permute-start.6 = (f32[4,32,32]{1,2,0:T(8,128)S(1)}, f32[4,32,32]{1,2,0:T(8,128)S(1)}, u32[]{:S(2)}, u32[]{:S(2)}) collective-permute-start(f32[4,32,32]{1,2,0:T(8,128)S(1)} %slice.62), channel_id=1, source_target_pairs={{0,1},{1,0},{2,3},{3,2},{4,5},{5,4},{6,7},{7,6},{8,9},{9,8},{10,11... | collective-permute-start | bytes 49160 | tf_op jit(solution)/shard_map/ppermute | solution.py:109
  24.0 38.2 %collective-permute-start.5 = (f32[4,32,32]{1,2,0:T(8,128)S(1)}, f32[4,32,32]{1,2,0:T(8,128)S(1)}, u32[]{:S(2)}, u32[]{:S(2)}) collective-permute-start(f32[4,32,32]{1,2,0:T(8,128)S(1)} %bitcast.233), channel_id=1, source_target_pairs={{0,2},{1,3},{2,0},{3,1},{4,6},{5,7},{6,4},{7,5},{8,10},{9,11},{10,... | collective-permute-start | bytes 49160 | tf_op jit(solution)/shard_map/ppermute | solution.py:108
  60.7 46.5 %collective-permute-start.18 = (bf16[4,64,4096]{2,1,0:T(8,128)(2,1)}, bf16[4,64,4096]{2,1,0:T(8,128)(2,1)}, u32[]{:S(2)}, u32[]{:S(2)}) collective-permute-start(bf16[4,64,4096]{2,1,0:T(8,128)(2,1)} %bitcast_dynamic-update-slice_fusion.6), channel_id=1, source_target_pairs={{0,1},{1,0},{2,3},{3,2},{4,5},{5,4},{6,7},{7,6},{8,9},{9,8},{10,11... | collective-permute-start | bytes 6291464 | tf_op jit(solution)/shard_map/ppermute | solution.py:105
  61.9 46.9 %collective-permute-start.19 = (bf16[4,64,4096]{2,1,0:T(8,128)(2,1)}, bf16[4,64,4096]{2,1,0:T(8,128)(2,1)}, u32[]{:S(2)}, u32[]{:S(2)}) collective-permute-start(bf16[4,64,4096]{2,1,0:T(8,128)(2,1)} %bitcast_dynamic-update-slice_fusion.6), channel_id=1, source_target_pairs={{0,2},{1,3},{2,0},{3,1},{4,6},{5,7},{6,4},{7,5},{8,10},{9,11},{10,... | collective-permute-start | bytes 6291464 | tf_op jit(solution)/shard_map/ppermute | solution.py:106
  108.5 22.9 %collective-permute-start.20 = (bf16[4,32,4096]{2,1,0:T(8,128)(2,1)S(1)}, bf16[4,32,4096]{2,1,0:T(8,128)(2,1)S(1)}, u32[]{:S(2)}, u32[]{:S(2)}) collective-permute-start(bf16[4,32,4096]{2,1,0:T(8,128)(2,1)S(1)} %slice.69), channel_id=1, source_target_pairs={{0,2},{1,3},{2,0},{3,1},{4,6},{5,7},{6,4},{7,5},{8,10},{9,11},{10,... | collective-permute-start | bytes 3145736 | tf_op jit(solution)/shard_map/ppermute | solution.py:108
  110.1 22.6 %collective-permute-start.21 = (bf16[4,32,4096]{2,1,0:T(8,128)(2,1)S(1)}, bf16[4,32,4096]{2,1,0:T(8,128)(2,1)S(1)}, u32[]{:S(2)}, u32[]{:S(2)}) collective-permute-start(bf16[4,32,4096]{2,1,0:T(8,128)(2,1)S(1)} %slice.70), channel_id=1, source_target_pairs={{0,1},{1,0},{2,3},{3,2},{4,5},{5,4},{6,7},{7,6},{8,9},{9,8},{10,11... | collective-permute-start | bytes 3145736 | tf_op jit(solution)/shard_map/ppermute | solution.py:109
  134.0 7.2 %copy-start.5 = (bf16[16,48,2048]{2,1,0:T(8,128)(2,1)}, bf16[16,48,2048]{2,1,0:T(8,128)(2,1)S(1)}, u32[]{:S(2)}) copy-start(bf16[16,48,2048]{2,1,0:T(8,128)(2,1)S(1)} %fusion.8) | copy-start | bytes 9437188
  134.0 3.0 copy-start.13
  137.0 4.1 %copy-start.14 = (bf16[1,1,2048,768]{3,2,1,0:T(8,128)(2,1)S(1)}, bf16[1,1,2048,768]{3,2,1,0:T(8,128)(2,1)}, u32[]{:S(2)}) copy-start(bf16[1,1,2048,768]{3,2,1,0:T(8,128)(2,1)} %param.19) | copy-start | bytes 9437188
  165.6 4.8 %copy-start.9 = (s32[1,64,8]{1,2,0:T(8,128)S(1)}, s32[1,64,8]{1,2,0:T(8,128)}, u32[]{:S(2)}) copy-start(s32[1,64,8]{1,2,0:T(8,128)} %param.16) | copy-start | bytes 6148
  165.6 6.7 %copy-start.2 = (bf16[1,64,2048]{2,1,0:T(8,128)(2,1)S(1)}, bf16[1,64,2048]{2,1,0:T(8,128)(2,1)}, u32[]{:S(2)}) copy-start(bf16[1,64,2048]{2,1,0:T(8,128)(2,1)} %param.11) | copy-start | bytes 786436
  165.6 75.5 %all-to-all-start.1 = ((bf16[16,48,2048]{2,1,0:T(8,128)(2,1)}), bf16[16,48,2048]{2,1,0:T(8,128)(2,1)}, u32[]{:S(2)}, u32[]{:S(2)}) async-start(bf16[16,48,2048]{2,1,0:T(8,128)(2,1)} %bitcast.223), calls=%async_computation.1 | async-start | bytes 6291456 | tf_op jit(solution)/shard_map/all_to_all | solution.py:170
  241.1 4.4 %copy-start.1 = (bf16[1,64,2048]{2,1,0:T(8,128)(2,1)S(1)}, bf16[1,64,2048]{2,1,0:T(8,128)(2,1)}, u32[]{:S(2)}) copy-start(bf16[1,64,2048]{2,1,0:T(8,128)(2,1)} %param.14) | copy-start | bytes 786436
  241.1 4.4 %copy-start.3 = (bf16[1,64,2048]{2,1,0:T(8,128)(2,1)S(1)}, bf16[1,64,2048]{2,1,0:T(8,128)(2,1)}, u32[]{:S(2)}) copy-start(bf16[1,64,2048]{2,1,0:T(8,128)(2,1)} %param.11) | copy-start | bytes 786436
  245.5 2.7 copy-start.7
  246.2 6.5 %collective-permute-start.7 = (bf16[64,2048]{1,0:T(8,128)(2,1)S(1)}, bf16[64,2048]{1,0:T(8,128)(2,1)S(1)}, u32[]{:S(2)}, u32[]{:S(2)}) collective-permute-start(bf16[64,2048]{1,0:T(8,128)(2,1)S(1)} %get-tuple-element.6), channel_id=1, source_target_pairs={{0,4},{1,5},{2,6},{3,7},{4,8},{5,9},{6,10},{7,11},{8,12},{9,13},{1... | collective-permute-start | bytes 786440 | tf_op jit(solution)/shard_map/ppermute | solution.py:101
  248.1 19.5 %collective-permute-start.8 = (bf16[64,2048]{1,0:T(8,128)(2,1)S(1)}, bf16[64,2048]{1,0:T(8,128)(2,1)S(1)}, u32[]{:S(2)}, u32[]{:S(2)}) collective-permute-start(bf16[64,2048]{1,0:T(8,128)(2,1)S(1)} %get-tuple-element.6), channel_id=1, source_target_pairs={{0,8},{1,9},{2,10},{3,11},{4,12},{5,13},{6,14},{7,15},{8,0},{9,1},... | collective-permute-start | bytes 786440 | tf_op jit(solution)/shard_map/ppermute | solution.py:101
  248.1 21.6 %collective-permute-start.9 = (bf16[64,2048]{1,0:T(8,128)(2,1)S(1)}, bf16[64,2048]{1,0:T(8,128)(2,1)S(1)}, u32[]{:S(2)}, u32[]{:S(2)}) collective-permute-start(bf16[64,2048]{1,0:T(8,128)(2,1)S(1)} %get-tuple-element.6), channel_id=1, source_target_pairs={{0,12},{1,13},{2,14},{3,15},{4,0},{5,1},{6,2},{7,3},{8,4},{9,5},{1... | collective-permute-start | bytes 786440 | tf_op jit(solution)/shard_map/ppermute | solution.py:101
  270.4 24.4 %collective-permute-start.10 = (bf16[4,64,2048]{2,1,0:T(8,128)(2,1)}, bf16[4,64,2048]{2,1,0:T(8,128)(2,1)}, u32[]{:S(2)}, u32[]{:S(2)}) collective-permute-start(bf16[4,64,2048]{2,1,0:T(8,128)(2,1)} %bitcast_dynamic-update-slice_fusion.10), channel_id=1, source_target_pairs={{0,1},{1,0},{2,3},{3,2},{4,5},{5,4},{6,7},{7,6},{8,9},{9,8},{10,11... | collective-permute-start | bytes 3145736 | tf_op jit(solution)/shard_map/ppermute | solution.py:105
  270.7 25.3 %collective-permute-start.11 = (bf16[4,64,2048]{2,1,0:T(8,128)(2,1)}, bf16[4,64,2048]{2,1,0:T(8,128)(2,1)}, u32[]{:S(2)}, u32[]{:S(2)}) collective-permute-start(bf16[4,64,2048]{2,1,0:T(8,128)(2,1)} %bitcast_dynamic-update-slice_fusion.10), channel_id=1, source_target_pairs={{0,2},{1,3},{2,0},{3,1},{4,6},{5,7},{6,4},{7,5},{8,10},{9,11},{10,... | collective-permute-start | bytes 3145736 | tf_op jit(solution)/shard_map/ppermute | solution.py:106
  295.9 12.1 %collective-permute-start.12 = (bf16[4,32,2048]{2,1,0:T(8,128)(2,1)S(1)}, bf16[4,32,2048]{2,1,0:T(8,128)(2,1)S(1)}, u32[]{:S(2)}, u32[]{:S(2)}) collective-permute-start(bf16[4,32,2048]{2,1,0:T(8,128)(2,1)S(1)} %slice.64), channel_id=1, source_target_pairs={{0,2},{1,3},{2,0},{3,1},{4,6},{5,7},{6,4},{7,5},{8,10},{9,11},{10,... | collective-permute-start | bytes 1572872 | tf_op jit(solution)/shard_map/ppermute | solution.py:108
  297.1 12.1 %collective-permute-start.13 = (bf16[4,32,2048]{2,1,0:T(8,128)(2,1)S(1)}, bf16[4,32,2048]{2,1,0:T(8,128)(2,1)S(1)}, u32[]{:S(2)}, u32[]{:S(2)}) collective-permute-start(bf16[4,32,2048]{2,1,0:T(8,128)(2,1)S(1)} %slice.65), channel_id=1, source_target_pairs={{0,1},{1,0},{2,3},{3,2},{4,5},{5,4},{6,7},{7,6},{8,9},{9,8},{10,11... | collective-permute-start | bytes 1572872 | tf_op jit(solution)/shard_map/ppermute | solution.py:109
  310.3 1.7 copy-start.6
  327.9 4.7 %copy-start.10 = (s32[1,64,8]{1,2,0:T(8,128)S(1)}, s32[1,64,8]{1,2,0:T(8,128)}, u32[]{:S(2)}) copy-start(s32[1,64,8]{1,2,0:T(8,128)} %param.12) | copy-start | bytes 6148
  327.9 7.4 %copy-start.12 = (f32[64]{0:T(128)S(1)}, f32[64]{0:T(128)}, u32[]{:S(2)}) copy-start(f32[64]{0:T(128)} %get-tuple-element.7) | copy-start | bytes 772
  327.9 74.0 %all-to-all-start = ((bf16[16,48,2048]{2,1,0:T(8,128)(2,1)}), bf16[16,48,2048]{2,1,0:T(8,128)(2,1)}, u32[]{:S(2)}, u32[]{:S(2)}) async-start(bf16[16,48,2048]{2,1,0:T(8,128)(2,1)} %bitcast.222), calls=%async_computation | async-start | bytes 6291456 | tf_op jit(solution)/shard_map/all_to_all | solution.py:163
  337.4 70.5 %collective-permute-start.22 = (bf16[1,64,2048]{2,1,0:T(8,128)(2,1)}, bf16[1,64,2048]{2,1,0:T(8,128)(2,1)S(1)}, u32[]{:S(2)}, u32[]{:S(2)}) collective-permute-start(bf16[1,64,2048]{2,1,0:T(8,128)(2,1)} %fusion.58), channel_id=1, source_target_pairs={{16,0},{0,16},{17,1},{1,17},{18,2},{2,18},{19,3},{3,19},{20,4},{4,... | collective-permute-start | bytes 786440 | tf_op jit(solution)/shard_map/ppermute | solution.py:12
  401.9 4.5 %copy-start.4 = (bf16[1,64,2048]{2,1,0:T(8,128)(2,1)S(1)}, bf16[1,64,2048]{2,1,0:T(8,128)(2,1)}, u32[]{:S(2)}) copy-start(bf16[1,64,2048]{2,1,0:T(8,128)(2,1)} %param.11) | copy-start | bytes 786436
  406.4 2.6 collective-permute-start.14

commit v4 on v3

--- a/solution.py
+++ b/solution.py
@@ -137,25 +137,33 @@
     weights_f = route_fwd[0] / jnp.sum(route_fwd[0], axis=-1, keepdims=True)
     weights_b = route_bwd[0] / jnp.sum(route_bwd[0], axis=-1, keepdims=True)
 
-    def gather(v):
-        return gather_ep(v, "ep")
-
-    tables = gather(
-        jnp.concatenate(
-            [ids_fwd[0].astype(jnp.float32), route_fwd[0], ids_bwd[0].astype(jnp.float32), route_bwd[0]],
-            axis=-1,
-        )
-    )
-    all_ids_f = tables[..., 0:top].astype(jnp.int32)
-    all_route_f = tables[..., top:2 * top]
-    all_ids_b = tables[..., 2 * top:3 * top].astype(jnp.int32)
-    all_route_b = tables[..., 3 * top:4 * top]
+    def split3(r):
+        hi = lax.reduce_precision(r, exponent_bits=8, mantissa_bits=7)
+        rest = r - hi
+        mid = lax.reduce_precision(rest, exponent_bits=8, mantissa_bits=7)
+        return jnp.concatenate([hi, mid, rest - mid], axis=-1).astype(jnp.bfloat16)
+
+    def join3(p):
+        p = p.astype(jnp.float32)
+        return (p[..., 0:top] + p[..., top:2 * top]) + p[..., 2 * top:3 * top]
+
+    meta = jnp.concatenate(
+        [ids_fwd[0].astype(jnp.bfloat16), ids_bwd[0].astype(jnp.bfloat16), split3(route_fwd[0]), split3(route_bwd[0])],
+        axis=-1,
+    )
+    pad = (-meta.shape[-1]) % 128
+    meta = jnp.concatenate([meta, jnp.zeros((tok_dev, pad), jnp.bfloat16)], axis=-1)
+    message = gather_ep(jnp.concatenate([h_f, h_b, grad, meta], axis=-1), "ep")
+    all_h_f = message[..., 0:width]
+    all_h_b = message[..., width:2 * width]
+    all_g = message[..., 2 * width:3 * width]
+    got = message[..., 3 * width:]
+    all_ids_f = got[..., 0:top].astype(jnp.int32)
+    all_ids_b = got[..., top:2 * top].astype(jnp.int32)
+    all_route_f = join3(got[..., 2 * top:5 * top])
+    all_route_b = join3(got[..., 5 * top:8 * top])
     all_w_f = all_route_f / jnp.sum(all_route_f, axis=-1, keepdims=True)
     all_w_b = all_route_b / jnp.sum(all_route_b, axis=-1, keepdims=True)
-    all_h_f = gather(h_f)
-    both_b = gather(jnp.concatenate([h_b, grad], axis=-1))
-    all_h_b = both_b[..., :width]
-    all_g = both_b[..., width:]
 
     onehot_f, _ = expert_slots(all_ids_f, all_w_f, me, cap)
     rows = pick_rows(onehot_f, all_h_f).reshape(-1, width)

time: 412 us -> 406 us (0.985)
  waiting for transfers between devices: 276 us -> 256 us
  starting transfers between devices: 27.5 us -> 20 us
  matrix products: 56.2 us -> 63.6 us
  local copies, waits for them, and re-layouts: 32.7 us -> 40.1 us
  other arithmetic: 17 us -> 24 us
    all_to_all x1, waiting for transfers between devices: 68.7 us -> 49.7 us  [local(): lax.all_to_all(made_b, 'ep', split_axis=0, concat_axis=0, tiled=True)]
    ppermute x9 -> x3, waiting for transfers between devices: 50.5 us -> 61.8 us  [gather_ep(): got = lax.ppermute(v, axis_name, _pairs(n, n2, 1, lambda a: (a + d) % n1))]
    dot_general x3, matrix products: 2.91 us -> 10.4 us  [pick_rows(): jnp.einsum('bct,btd->bcd', onehot, rows, preferred_element_type=jnp.float32)]
    div x1, other arithmetic: 0.05 us -> 6.41 us  [local(): all_w_b = all_route_b / jnp.sum(all_route_b, axis=-1, keepdims=True)]
    ppermute x9 -> x3, starting transfers between devices: 8.47 us -> 3.77 us  [gather_ep(): got = lax.ppermute(v, axis_name, _pairs(n, n2, 1, lambda a: (a + d) % n1))]
    broadcast_in_dim x3 -> x1, local copies, waits for them, and re-layouts: 1.57 us -> 6.23 us  [gather_ep(): s2 = jnp.zeros((n2,) + s1.shape, v.dtype)]
    ppermute x3 -> x1, waiting for transfers between devices: 63.5 us -> 59.1 us  [gather_ep(): px = lax.ppermute(s1, axis_name, _pairs(n, n2, 2, flip_x))]
    ppermute x3 -> x1, waiting for transfers between devices: 24.5 us -> 24.3 us  [gather_ep(): d1 = lax.ppermute(px[:, :h], axis_name, _pairs(n, n2, 2, flip_y))]
  transfers between devices with their start and end apart: 25 -> 11, of which waited for: 15 -> 9; matrix products, arithmetic and copies ran while one was open for 11% -> 15% of each run, Pallas kernels for 0% -> 0%
where the time goes in v4:
time: 406 us; the launch traced here: 405 us
  waiting for transfers between devices  256 us (63%)
  matrix products  63.6 us (16%)
  local copies, waits for them, and re-layouts  40.1 us (10%)
  other arithmetic  24 us (6%)
  starting transfers between devices  20 us (5%)
    ppermute x3, waiting for transfers between devices, gather_ep(): got = lax.ppermute(v, axis_name, _pairs(n, n2, 1, lambda a: (a + d) % n1))  61.8 us
    ppermute x1, waiting for transfers between devices, gather_ep(): px = lax.ppermute(s1, axis_name, _pairs(n, n2, 2, flip_x))  59.1 us
    all_to_all x1, waiting for transfers between devices, local(): lax.all_to_all(made_f, 'ep', split_axis=0, concat_axis=0, tiled=True)  58.8 us
    all_to_all x1, waiting for transfers between devices, local(): lax.all_to_all(made_b, 'ep', split_axis=0, concat_axis=0, tiled=True)  49.7 us
    ppermute x1, waiting for transfers between devices, gather_ep(): d1 = lax.ppermute(px[:, :h], axis_name, _pairs(n, n2, 2, flip_y))  24.3 us
    dot_general x1, matrix products, expert_backward(): jnp.dot(dgate, w_g.T, preferred_element_type=jnp.float32)  12.9 us
    dot_general x1, matrix products, expert_forward(): jnp.dot(act, w_d, preferred_element_type=jnp.float32).astype(jnp.bfloat16)  11.9 us
    dot_general x3, matrix products, pick_rows(): jnp.einsum('bct,btd->bcd', onehot, rows, preferred_element_type=jnp.float32)  10.4 us
  transfers between devices with their start and end apart: 11, of which 9 were waited for; matrix products, arithmetic and copies ran while one was open for 15% of the time, Pallas kernels for 0%

profile of v4, /device:TPU:13, one launch (start us, length us, event | category | flops | bytes accessed | tf_op | source)
XLA Modules:
  0.0 404.9 jit_solution(13965254821809151938)
XLA Ops:
  0.6 1.3 fusion.55
  1.9 1.1 fusion.59
  3.0 0.7 mul.218
  3.7 0.8 copy.38
  4.5 0.8 copy.43
  5.3 0.7 reduce_sum.107
  6.0 0.7 bitcast_divide_fusion
  7.0 0.7 fusion.90
  7.8 0.7 copy.48
  8.5 0.7 copy.49
  9.7 0.6 convert_bitcast_fusion.2
  10.3 1.9 fusion.61
  12.2 0.6 broadcast_in_dim.78
  12.8 2.0 concatenate.11
  14.8 1.3 collective-permute-start
  16.1 1.1 collective-permute-start.1
  17.2 1.4 collective-permute-start.2
  18.6 1.9 broadcast_in_dim.77
  20.6 0.9 bitcast_dynamic-update-slice_fusion.6
  21.5 12.4 %collective-permute-done = bf16[64,6272]{1,0:T(8,128)(2,1)} collective-permute-done((bf16[64,6272]{1,0:T(8,128)(2,1)}, bf16[64,6272]{1,0:T(8,128)(2,1)}, u32[]{:S(2)}, u32[]{:S(2)}) %collective-permute-start) | collective-permute-done | bytes 802848 | tf_op jit(solution)/shard_map/ppermute | solution.py:101
  33.9 2.1 bitcast_dynamic-update-slice_fusion.5
  36.0 48.6 %collective-permute-done.1 = bf16[64,6272]{1,0:T(8,128)(2,1)} collective-permute-done((bf16[64,6272]{1,0:T(8,128)(2,1)}, bf16[64,6272]{1,0:T(8,128)(2,1)}, u32[]{:S(2)}, u32[]{:S(2)}) %collective-permute-start.1) | collective-permute-done | bytes 802848 | tf_op jit(solution)/shard_map/ppermute | solution.py:101
  84.6 2.1 bitcast_dynamic-update-slice_fusion.4
  86.7 0.7 collective-permute-done.2
  87.5 2.1 bitcast_dynamic-update-slice_fusion.3
  89.5 1.2 collective-permute-start.3
  91.0 6.2 %broadcast_in_dim.76 = bf16[4,4,64,6272]{3,2,0,1:T(8,128)(2,1)} broadcast(bf16[]{:T(256)} %constant.89.clone.1), dimensions={} | broadcast | bytes 12845058 | tf_op jit(solution)/shard_map/broadcast_in_dim | solution.py:111
  97.2 3.8 bitcast_dynamic-update-slice_fusion.2
  101.0 59.1 %collective-permute-done.3 = bf16[4,64,6272]{2,1,0:T(8,128)(2,1)} collective-permute-done((bf16[4,64,6272]{2,1,0:T(8,128)(2,1)}, bf16[4,64,6272]{2,1,0:T(8,128)(2,1)}, u32[]{:S(2)}, u32[]{:S(2)}) %collective-permute-start.3) | collective-permute-done | bytes 3211296 | tf_op jit(solution)/shard_map/ppermute | solution.py:105
  160.1 1.5 slice.65
  161.9 1.5 slice.66
  163.5 1.3 collective-permute-start.6
  164.7 3.8 bitcast_dynamic-update-slice_fusion.1
  168.6 3.8 bitcast_dynamic-update-slice_fusion
  172.4 24.3 %collective-permute-done.5 = bf16[4,32,6272]{2,1,0:T(8,128)(2,1)S(1)} collective-permute-done((bf16[4,32,6272]{2,1,0:T(8,128)(2,1)S(1)}, bf16[4,32,6272]{2,1,0:T(8,128)(2,1)S(1)}, u32[]{:S(2)}, u32[]{:S(2)}) %collective-permute-start.5) | collective-permute-done | bytes 1605664 | tf_op jit(solution)/shard_map/ppermute | solution.py:108
  196.7 1.5 collective-permute-done.6
  198.2 1.9 fusion.16
  200.2 1.1 slice_convert_fusion
  201.3 1.9 fusion.88
  203.2 6.4 %fusion.95 = f32[16,64]{1,0:T(8,128)S(1)} fusion(f32[16,64,24]{2,1,0:T(8,128)S(1)} %slice_convert_fusion, s32[]{:T(128)S(6)} %axis_index.16, bf16[16,64,6272]{2,1,0:T(8,128)(2,1)} %bitcast.179), kind=kOutput, calls=%fused_computation.135 | output fusion | flops 57351 | bytes 1593348 | tf_op jit(solution)/shard_map/div | solution.py:166
  209.8 3.1 fusion.13
  213.2 4.1 %multiply_convert_fusion = bf16[16,48,2048]{2,1,0:T(8,128)(2,1)S(1)} fusion(f32[16,48]{1,0:T(8,128)S(1)} %select_reduce_fusion, bf16[16,64,6272]{2,1,0:T(8,128)(2,1)} %bitcast.181, s32[16,64]{1,0:T(8,128)S(1)} %convert_subtract_fusion, pred[16,64]{1,0:T(8,128)(4,1)S(1)} %get-tuple-element.2), kind=kOutput, calls=%fused_computation.2 | convolution fusion | flops 207716352 | bytes 7348224 | tf_op jit(solution)/shard_map/bct,btd->bcd/dot_general | solution.py:67
  217.3 4.1 %fusion.17 = f32[768,768]{1,0:T(8,128)} fusion(bf16[768,2048]{1,0:T(8,128)(2,1)S(1)} %bitcast.189, bf16[1,1,768,2048]{3,2,1,0:T(8,128)(2,1)S(1)} %copy-done.8), kind=kOutput, calls=%fused_computation.19 | convolution fusion | flops 2415919104 | bytes 8650752 | tf_op jit(solution)/shard_map/dot_general | solution.py:40
  221.4 4.0 fusion.27
  225.5 12.9 %fusion.25 = f32[768,2048]{1,0:T(8,128)} fusion(bf16[1,1,2048,768]{3,2,1,0:T(8,128)(2,1)} %param.19, f32[768,768]{1,0:T(8,128)} %fusion.27, f32[768,768]{1,0:T(8,128)} %fusion.17, bf16[768,2048]{1,0:T(8,128)(2,1)} %bitcast.184, bf16[1,1,2048,768]{3,2,1,0:T(8,128)(2,1)S(1)} %copy-done), kind=kOutput, calls=%fused_computation.27 | convolution fusion | flops 4837736448 | bytes 20447232 | tf_op jit(solution)/shard_map/dot_general | solution.py:43
  238.3 7.4 %add_convert_fusion = bf16[768,2048]{1,0:T(8,128)(2,1)} fusion(f32[768,2048]{1,0:T(8,128)} %fusion.25, bf16[1,1,2048,768]{3,2,1,0:T(8,128)(2,1)S(1)} %copy-done, f32[768,768]{1,0:T(8,128)} %fusion.17, f32[768,768]{1,0:T(8,128)} %fusion.27), kind=kOutput, calls=%fused_computation.1 | convolution fusion | flops 2422603776 | bytes 17301504 | tf_op jit(solution)/shard_map/dot_general | solution.py:43
  245.8 5.3 %all-to-all-start.1 = ((bf16[16,48,2048]{2,1,0:T(8,128)(2,1)}), bf16[16,48,2048]{2,1,0:T(8,128)(2,1)}, u32[]{:S(2)}, u32[]{:S(2)}) async-start(bf16[16,48,2048]{2,1,0:T(8,128)(2,1)} %bitcast.188), calls=%async_computation.1 | async-start | bytes 6291456 | tf_op jit(solution)/shard_map/all_to_all | solution.py:178
  251.3 3.1 fusion.7
  254.5 1.7 copy-done.4
  256.1 4.0 fusion.23
  260.2 11.9 %convolution_convert_fusion = bf16[768,2048]{1,0:T(8,128)(2,1)} fusion(bf16[1,1,768,2048]{3,2,1,0:T(8,128)(2,1)} %param.21, f32[768,768]{1,0:T(8,128)} %fusion.23, bf16[768,2048]{1,0:T(8,128)(2,1)} %bitcast.186, bf16[1,1,2048,768]{3,2,1,0:T(8,128)(2,1)} %param.19), kind=kOutput, calls=%fused_computation.13 | convolution fusion | flops 4836950016 | bytes 14942208 | tf_op jit(solution)/shard_map/dot_general | solution.py:33
  272.0 49.7 %all-to-all-done.1 = bf16[16,48,2048]{2,1,0:T(8,128)(2,1)} async-done(((bf16[16,48,2048]{2,1,0:T(8,128)(2,1)}), bf16[16,48,2048]{2,1,0:T(8,128)(2,1)}, u32[]{:S(2)}, u32[]{:S(2)}) %all-to-all-start.1) | async-done | bytes 3145760 | tf_op jit(solution)/shard_map/all_to_all | solution.py:178
  321.8 4.6 %all-to-all-start = ((bf16[16,48,2048]{2,1,0:T(8,128)(2,1)}), bf16[16,48,2048]{2,1,0:T(8,128)(2,1)}, u32[]{:S(2)}, u32[]{:S(2)}) async-start(bf16[16,48,2048]{2,1,0:T(8,128)(2,1)} %bitcast.187), calls=%async_computation | async-start | bytes 6291456 | tf_op jit(solution)/shard_map/all_to_all | solution.py:171
  326.8 1.2 reduce-window.16
  328.4 1.2 reduce-window.14
  330.1 4.4 %convolution_reduce_fusion = f32[64,2048]{1,0:T(8,128)S(1)} fusion(bf16[768,2048,1]{1,0,2:T(8,128)(2,1)} %bitcast.40, s32[64,8]{1,0:T(8,128)S(1)} %bitcast_add_fusion), kind=kOutput, calls=%fused_computation.37 | convolution fusion | flops 1611923456 | bytes 3672064 | tf_op jit(solution)/shard_map/dot_general | solution.py:74
  334.7 1.0 fusion.66
  335.7 1.9 collective-permute-start.8
  337.5 58.8 %all-to-all-done = bf16[16,48,2048]{2,1,0:T(8,128)(2,1)} async-done(((bf16[16,48,2048]{2,1,0:T(8,128)(2,1)}), bf16[16,48,2048]{2,1,0:T(8,128)(2,1)}, u32[]{:S(2)}, u32[]{:S(2)}) %all-to-all-start) | async-done | bytes 3145760 | tf_op jit(solution)/shard_map/all_to_all | solution.py:171
  396.3 4.5 %multiply_reduce_fusion = f32[64,2048]{1,0:T(8,128)S(1)} fusion(bf16[768,2048,1]{1,0,2:T(8,128)(2,1)} %bitcast.31, f32[64,8]{1,0:T(8,128)S(1)} %copy.37, s32[64,8]{1,0:T(8,128)S(1)} %bitcast_add_fusion.1), kind=kOutput, calls=%fused_computation.9 | convolution fusion | flops 1612972032 | bytes 3674112 | tf_op jit(solution)/shard_map/dot_general | solution.py:74
  400.9 1.5 collective-permute-start.7
  402.3 1.2 collective-permute-done.7
  403.5 0.7 copy.71
  404.2 0.7 copy.72
  (57 shorter events, 3.8 us)
Async XLA Ops:
  0.6 224.8 %copy-start = (bf16[1,1,2048,768]{3,2,1,0:T(8,128)(2,1)S(1)}, bf16[1,1,2048,768]{3,2,1,0:T(8,128)(2,1)}, u32[]{:S(2)}) copy-start(bf16[1,1,2048,768]{3,2,1,0:T(8,128)(2,1)} %param.20) | copy-start | bytes 9437188
  14.8 19.1 %collective-permute-start = (bf16[64,6272]{1,0:T(8,128)(2,1)}, bf16[64,6272]{1,0:T(8,128)(2,1)}, u32[]{:S(2)}, u32[]{:S(2)}) collective-permute-start(bf16[64,6272]{1,0:T(8,128)(2,1)} %concatenate.11), channel_id=1, source_target_pairs={{0,4},{1,5},{2,6},{3,7},{4,8},{5,9},{6,10},{7,11},{8,12},{9,13},{1... | collective-permute-start | bytes 2408456 | tf_op jit(solution)/shard_map/ppermute | solution.py:101
  16.1 68.5 %collective-permute-start.1 = (bf16[64,6272]{1,0:T(8,128)(2,1)}, bf16[64,6272]{1,0:T(8,128)(2,1)}, u32[]{:S(2)}, u32[]{:S(2)}) collective-permute-start(bf16[64,6272]{1,0:T(8,128)(2,1)} %concatenate.11), channel_id=1, source_target_pairs={{0,8},{1,9},{2,10},{3,11},{4,12},{5,13},{6,14},{7,15},{8,0},{9,1},... | collective-permute-start | bytes 2408456 | tf_op jit(solution)/shard_map/ppermute | solution.py:101
  17.2 70.3 %collective-permute-start.2 = (bf16[64,6272]{1,0:T(8,128)(2,1)}, bf16[64,6272]{1,0:T(8,128)(2,1)}, u32[]{:S(2)}, u32[]{:S(2)}) collective-permute-start(bf16[64,6272]{1,0:T(8,128)(2,1)} %concatenate.11), channel_id=1, source_target_pairs={{0,12},{1,13},{2,14},{3,15},{4,0},{5,1},{6,2},{7,3},{8,4},{9,5},{1... | collective-permute-start | bytes 2408456 | tf_op jit(solution)/shard_map/ppermute | solution.py:101
  18.6 2.0 copy-start.2
  89.5 70.6 %collective-permute-start.3 = (bf16[4,64,6272]{2,1,0:T(8,128)(2,1)}, bf16[4,64,6272]{2,1,0:T(8,128)(2,1)}, u32[]{:S(2)}, u32[]{:S(2)}) collective-permute-start(bf16[4,64,6272]{2,1,0:T(8,128)(2,1)} %bitcast_dynamic-update-slice_fusion.3), channel_id=1, source_target_pairs={{0,1},{1,0},{2,3},{3,2},{4,5},{5,4},{6,7},{7,6},{8,9},{9,8},{10,11... | collective-permute-start | bytes 9633800 | tf_op jit(solution)/shard_map/ppermute | solution.py:105
  90.7 71.2 %collective-permute-start.4 = (bf16[4,64,6272]{2,1,0:T(8,128)(2,1)}, bf16[4,64,6272]{2,1,0:T(8,128)(2,1)}, u32[]{:S(2)}, u32[]{:S(2)}) collective-permute-start(bf16[4,64,6272]{2,1,0:T(8,128)(2,1)} %bitcast_dynamic-update-slice_fusion.3), channel_id=1, source_target_pairs={{0,2},{1,3},{2,0},{3,1},{4,6},{5,7},{6,4},{7,5},{8,10},{9,11},{10,... | collective-permute-start | bytes 9633800 | tf_op jit(solution)/shard_map/ppermute | solution.py:106
  161.6 35.0 %collective-permute-start.5 = (bf16[4,32,6272]{2,1,0:T(8,128)(2,1)S(1)}, bf16[4,32,6272]{2,1,0:T(8,128)(2,1)S(1)}, u32[]{:S(2)}, u32[]{:S(2)}) collective-permute-start(bf16[4,32,6272]{2,1,0:T(8,128)(2,1)S(1)} %slice.65), channel_id=1, source_target_pairs={{0,2},{1,3},{2,0},{3,1},{4,6},{5,7},{6,4},{7,5},{8,10},{9,11},{10,... | collective-permute-start | bytes 4816904 | tf_op jit(solution)/shard_map/ppermute | solution.py:108
  163.5 34.8 %collective-permute-start.6 = (bf16[4,32,6272]{2,1,0:T(8,128)(2,1)S(1)}, bf16[4,32,6272]{2,1,0:T(8,128)(2,1)S(1)}, u32[]{:S(2)}, u32[]{:S(2)}) collective-permute-start(bf16[4,32,6272]{2,1,0:T(8,128)(2,1)S(1)} %slice.66), channel_id=1, source_target_pairs={{0,1},{1,0},{2,3},{3,2},{4,5},{5,4},{6,7},{7,6},{8,9},{9,8},{10,11... | collective-permute-start | bytes 4816904 | tf_op jit(solution)/shard_map/ppermute | solution.py:109
  213.0 8.5 %copy-start.3 = (bf16[16,48,2048]{2,1,0:T(8,128)(2,1)}, bf16[16,48,2048]{2,1,0:T(8,128)(2,1)S(1)}, u32[]{:S(2)}) copy-start(bf16[16,48,2048]{2,1,0:T(8,128)(2,1)S(1)} %fusion.13) | copy-start | bytes 9437188
  213.2 4.1 %copy-start.8 = (bf16[1,1,768,2048]{3,2,1,0:T(8,128)(2,1)S(1)}, bf16[1,1,768,2048]{3,2,1,0:T(8,128)(2,1)}, u32[]{:S(2)}) copy-start(bf16[1,1,768,2048]{3,2,1,0:T(8,128)(2,1)} %param.21) | copy-start | bytes 9437188
  217.3 4.1 %copy-start.9 = (bf16[1,1,2048,768]{3,2,1,0:T(8,128)(2,1)S(1)}, bf16[1,1,2048,768]{3,2,1,0:T(8,128)(2,1)}, u32[]{:S(2)}) copy-start(bf16[1,1,2048,768]{3,2,1,0:T(8,128)(2,1)} %param.19) | copy-start | bytes 9437188
  245.8 76.0 %all-to-all-start.1 = ((bf16[16,48,2048]{2,1,0:T(8,128)(2,1)}), bf16[16,48,2048]{2,1,0:T(8,128)(2,1)}, u32[]{:S(2)}, u32[]{:S(2)}) async-start(bf16[16,48,2048]{2,1,0:T(8,128)(2,1)} %bitcast.188), calls=%async_computation.1 | async-start | bytes 6291456 | tf_op jit(solution)/shard_map/all_to_all | solution.py:178
  254.4 1.7 copy-start.4
  321.8 74.5 %all-to-all-start = ((bf16[16,48,2048]{2,1,0:T(8,128)(2,1)}), bf16[16,48,2048]{2,1,0:T(8,128)(2,1)}, u32[]{:S(2)}, u32[]{:S(2)}) async-start(bf16[16,48,2048]{2,1,0:T(8,128)(2,1)} %bitcast.187), calls=%async_computation | async-start | bytes 6291456 | tf_op jit(solution)/shard_map/all_to_all | solution.py:171
  330.1 4.4 %copy-start.1 = (bf16[1,64,2048]{2,1,0:T(8,128)(2,1)S(1)}, bf16[1,64,2048]{2,1,0:T(8,128)(2,1)}, u32[]{:S(2)}) copy-start(bf16[1,64,2048]{2,1,0:T(8,128)(2,1)} %param.14) | copy-start | bytes 786436
  330.1 4.6 %copy-start.6 = (bf16[1,64,2048]{2,1,0:T(8,128)(2,1)S(1)}, bf16[1,64,2048]{2,1,0:T(8,128)(2,1)}, u32[]{:S(2)}) copy-start(bf16[1,64,2048]{2,1,0:T(8,128)(2,1)} %param.15) | copy-start | bytes 786436
  330.1 4.6 %copy-start.7 = (f32[64]{0:T(128)S(1)}, f32[64]{0:T(128)}, u32[]{:S(2)}) copy-start(f32[64]{0:T(128)} %get-tuple-element.13) | copy-start | bytes 772
  335.7 66.7 %collective-permute-start.8 = (bf16[1,64,2048]{2,1,0:T(8,128)(2,1)}, bf16[1,64,2048]{2,1,0:T(8,128)(2,1)S(1)}, u32[]{:S(2)}, u32[]{:S(2)}) collective-permute-start(bf16[1,64,2048]{2,1,0:T(8,128)(2,1)} %fusion.66), channel_id=1, source_target_pairs={{16,0},{0,16},{17,1},{1,17},{18,2},{2,18},{19,3},{3,19},{20,4},{4,... | collective-permute-start | bytes 786440 | tf_op jit(solution)/shard_map/ppermute | solution.py:12
  396.3 4.5 %copy-start.5 = (bf16[1,64,2048]{2,1,0:T(8,128)(2,1)S(1)}, bf16[1,64,2048]{2,1,0:T(8,128)(2,1)}, u32[]{:S(2)}) copy-start(bf16[1,64,2048]{2,1,0:T(8,128)(2,1)} %param.11) | copy-start | bytes 786436
  400.9 2.6 collective-permute-start.7
